TPU v7x, 32 devices: a whole 2x2x4 slice. The times are simulated.
32 devices in a mesh: rows: 16 (over z, y, x), grp: 2 (over core).
Axes of the slice: x: 2, y: 2, z: 4, core: 2. Of those that a mesh axis runs over, the one named last changes fastest.
Arguments:
- slab_x: bfloat16 [131072, 512], P(('rows', 'grp'))
- slab_y: bfloat16 [131072, 256], P(('rows', 'grp')), may hold values from -6 to 6
- row_mask: int32 [131072], P(('rows', 'grp')), may hold values 0 or 1
- live_tiles: int32 [32], P(('rows', 'grp')), may hold values from 1 to 32, as said below
- old_r: float32 [512, 512], P('rows'), as said below
- old_z: float32 [512, 256], P('rows'), may hold values from -6 to 6
Outputs:
- new_r: float32 [512, 512], replicated
- new_z: float32 [512, 256], replicated
Inputs may be any that keep to these rules, and one draw needn't show every extreme that they name: `live_tiles`: live tiles of each device; at least one device has all 32. old_r is upper triangular with diagonal entries from 0.5 to 2.
All inputs are finite; a program needn't handle non-finite values. No bound on the sum of `row_mask` on one device may be relied on, other than what follows from the above.
Results may differ from a plain program's by a relative error of at most 0.0003.
Values sent between devices are 32-bit elements; how exact they have to be, the bound alone decides.
No kernel may reach another device: no remote copies, remote signals or barrier semaphores. Data moves between devices by JAX's collectives and lax.ppermute only.
A program may use at most 64 MiB of HBM per device.

v0:
```python
import jax
import jax.numpy as jnp
from jax import lax
from jax.sharding import PartitionSpec as P

TILE = 128
AXES = ("rows", "grp")


def contract(left, right, precision=None):
    return lax.dot_general(
        left,
        right,
        (((0,), (0,)), ((), ())),
        precision=precision,
        preferred_element_type=jnp.float32,
    )


def digit_groups(n_dev):
    bits = n_dev.bit_length() - 1
    groups = [(0, 1)] if bits else []
    k = 1
    while k < bits:
        width = min(2, bits - k)
        groups.append((k, width))
        k += width
    return groups


def pick(pieces, digit):
    out = pieces[-1]
    for t in range(len(pieces) - 2, -1, -1):
        out = jnp.where(digit == t, pieces[t], out)
    return out


def exchange_sum(local, n_dev):
    idx = lax.axis_index(AXES)
    groups = digit_groups(n_dev)
    cur = local
    for k, width in groups:
        radix = 1 << width
        digit = (idx >> k) & (radix - 1)
        size = cur.shape[0] // radix
        parts = [cur[t * size : (t + 1) * size] for t in range(radix)]
        acc = pick(parts, digit)
        for a in range(1, radix):
            pairs = [(i, i ^ (a << k)) for i in range(n_dev)]
            acc = acc + lax.ppermute(pick(parts, digit ^ a), AXES, pairs)
        cur = acc
    for k, width in reversed(groups):
        radix = 1 << width
        digit = (idx >> k) & (radix - 1)
        got = [cur]
        for a in range(1, radix):
            pairs = [(i, i ^ (a << k)) for i in range(n_dev)]
            got.append(lax.ppermute(cur, AXES, pairs))
        cur = jnp.concatenate([pick(got, digit ^ t) for t in range(radix)], axis=0)
    return cur


def summed(local, n_dev):
    rows = local.shape[0]
    if n_dev & (n_dev - 1) == 0 and rows % n_dev == 0 and n_dev > 1:
        return exchange_sum(local, n_dev)
    return lax.psum(local, AXES)


def top_bits(v):
    t = v * 65537.0
    return t - (t - v)


def split3(v):
    hi = top_bits(v)
    rest = v - hi
    mid = top_bits(rest)
    lo = rest - mid
    return hi.astype(jnp.bfloat16), mid.astype(jnp.bfloat16), lo.astype(jnp.bfloat16)


def fine_product(left, right, axis):
    lh, lm, ll = split3(left)
    rh, rm, rl = split3(right)
    lefts = jnp.concatenate([lh, lh, lm, lh, lm, ll], axis=axis)
    rights = jnp.concatenate([rh, rm, rh, rl, rm, rh], axis=axis)
    return lax.dot_general(
        lefts, rights, (((axis,), (axis,)), ((), ())), preferred_element_type=jnp.float32
    )


def body(slab_x, slab_y, row_mask, live_tiles, old_r, old_z):
    rows_here, width = slab_x.shape
    n_grp = lax.axis_size("grp")
    n_dev = lax.axis_size("rows") * n_grp
    tile_ids = lax.broadcasted_iota(jnp.int32, (rows_here,), 0) // TILE
    live = (row_mask == 1) & (tile_ids < live_tiles[0])
    masked = jnp.where(live[:, None], slab_x, jnp.zeros_like(slab_x))
    gram = contract(masked, slab_x)
    cross = contract(masked, slab_y)
    share = old_r.shape[0] // n_grp
    start = lax.axis_index("grp") * share
    r_part = lax.dynamic_slice_in_dim(old_r, start, share, 0)
    z_part = lax.dynamic_slice_in_dim(old_z, start, share, 0)
    old = fine_product(r_part, jnp.concatenate([r_part, z_part], axis=1), 0)
    gram = gram + old[:, :width]
    cross = cross + old[:, width:]
    both = summed(jnp.concatenate([gram.T, cross.T], axis=0), n_dev)
    return factor_and_solve(both)


def factor_and_solve(trail, block=128):
    n = trail.shape[1]
    columns = []
    for s in range(0, n, block):
        diag = lax.linalg.cholesky(trail[:block, :block], symmetrize_input=False)
        panel = lax.linalg.triangular_solve(
            diag, trail[block:, :block], left_side=False, lower=True, transpose_a=True
        )
        columns.append(jnp.concatenate([diag, panel], axis=0))
        if s + block < n:
            upper = panel[: n - s - block]
            trail = trail[block:, block:] - lax.dot_general(
                panel,
                upper,
                (((1,), (1,)), ((), ())),
                precision=lax.Precision.HIGHEST,
                preferred_element_type=jnp.float32,
            )
    lower = jnp.concatenate(
        [jnp.pad(col[: n - s], ((s, 0), (0, 0))) for s, col in zip(range(0, n, block), columns)],
        axis=1,
    )
    new_z_t = jnp.concatenate([col[n - s :] for s, col in zip(range(0, n, block), columns)], axis=1)
    return (lower.T, new_z_t.T)


def solution(mesh):
    placed = (
        P(AXES, None),
        P(AXES, None),
        P(AXES),
        P(AXES),
        P("rows", None),
        P("rows", None),
    )
    return jax.shard_map(body, mesh=mesh, in_specs=placed, out_specs=(P(), P()), check_vma=False)
```

profile of v0, /device:TPU:0, one launch (start us, length us, event | category | flops | bytes accessed | tf_op | source)
XLA Modules:
  0.0 175.4 jit_solution(5539413658630064580)
XLA Ops:
  4.3 6.4 %fusion.11 = f32[512,512]{1,0:T(8,128)S(1)} fusion(bf16[4096,512]{1,0:T(8,128)(2,1)} %param.7, pred[4096]{0:T(1024)(128)(4,1)S(1)} %fusion.61, f32[512,768]{0,1:T(8,128)S(1)} %fusion.65), kind=kOutput, calls=%fused_computation.9 | convolution fusion | flops 2149842944 | bytes 10489856 | tf_op jit(solution)/shard_map/dot_general | solution.py:11
  10.8 2.6 %fusion.17 = f32[256,512]{1,0:T(8,128)} fusion(bf16[4096,256]{1,0:T(8,128)(2,1)S(1)} %copy-done, bf16[4096,512]{1,0:T(8,128)(2,1)S(1)} %copy-done.4, pred[4096]{0:T(1024)(128)(4,1)S(1)} %fusion.61, f32[512,768]{0,1:T(8,128)S(1)} %fusion.65), kind=kOutput, calls=%fused_computation.11 | convolution fusion | flops 1075970048 | bytes 7344128 | tf_op jit(solution)/shard_map/dot_general | solution.py:11
  13.4 2.1 %slice_select_fusion = f32[384,512]{1,0:T(8,128)} fusion(f32[512,512]{1,0:T(8,128)S(1)} %fusion.11, pred[]{:T(512)S(6)} %eq.115, f32[256,512]{1,0:T(8,128)} %fusion.17), kind=kLoop, calls=%fused_computation.24 | loop fusion | flops 393216 | bytes 3145729 | tf_op jit(solution)/shard_map/jit(_where)/select_n | solution.py:34
  15.9 2.3 %collective-permute-done = f32[384,512]{1,0:T(8,128)} collective-permute-done((f32[384,512]{1,0:T(8,128)}, f32[384,512]{1,0:T(8,128)}, u32[]{:S(2)}, u32[]{:S(2)}) %collective-permute-start) | collective-permute-done | bytes 786464 | tf_op jit(solution)/shard_map/ppermute | solution.py:50
  19.7 2.9 %collective-permute-start.1 = (f32[96,512]{1,0:T(8,128)S(1)}, f32[96,512]{1,0:T(8,128)S(1)}, u32[]{:S(2)}, u32[]{:S(2)}) collective-permute-start(f32[96,512]{1,0:T(8,128)S(1)} %get-tuple-element.21), channel_id=1, source_target_pairs={{0,2},{1,3},{2,0},{3,1},{4,6},{5,7},{6,4},{7,5},{8,10},{9,11},{10,... | collective-permute-start | bytes 589832 | tf_op jit(solution)/shard_map/ppermute | solution.py:50
  24.5 3.9 %collective-permute-done.1 = f32[96,512]{1,0:T(8,128)S(1)} collective-permute-done((f32[96,512]{1,0:T(8,128)S(1)}, f32[96,512]{1,0:T(8,128)S(1)}, u32[]{:S(2)}, u32[]{:S(2)}) %collective-permute-start.1) | collective-permute-done | bytes 196640 | tf_op jit(solution)/shard_map/ppermute | solution.py:50
  28.4 5.2 %collective-permute-done.2 = f32[96,512]{1,0:T(8,128)S(1)} collective-permute-done((f32[96,512]{1,0:T(8,128)S(1)}, f32[96,512]{1,0:T(8,128)S(1)}, u32[]{:S(2)}, u32[]{:S(2)}) %collective-permute-start.2) | collective-permute-done | bytes 196640 | tf_op jit(solution)/shard_map/ppermute | solution.py:50
  36.6 2.6 %collective-permute-start.5 = (f32[24,512]{1,0:T(8,128)S(1)}, f32[24,512]{1,0:T(8,128)S(1)}, u32[]{:S(2)}, u32[]{:S(2)}) collective-permute-start(f32[24,512]{1,0:T(8,128)S(1)} %get-tuple-element.28), channel_id=1, source_target_pairs={{0,16},{1,17},{2,18},{3,19},{4,20},{5,21},{6,22},{7,23},{8,24},{9,... | collective-permute-start | bytes 147464 | tf_op jit(solution)/shard_map/ppermute | solution.py:50
  39.5 2.6 %collective-permute-done.5 = f32[24,512]{1,0:T(8,128)S(1)} collective-permute-done((f32[24,512]{1,0:T(8,128)S(1)}, f32[24,512]{1,0:T(8,128)S(1)}, u32[]{:S(2)}, u32[]{:S(2)}) %collective-permute-start.5) | collective-permute-done | bytes 49184 | tf_op jit(solution)/shard_map/ppermute | solution.py:50
  42.1 3.3 %collective-permute-done.6 = f32[24,512]{1,0:T(8,128)S(1)} collective-permute-done((f32[24,512]{1,0:T(8,128)S(1)}, f32[24,512]{1,0:T(8,128)S(1)}, u32[]{:S(2)}, u32[]{:S(2)}) %collective-permute-start.6) | collective-permute-done | bytes 49184 | tf_op jit(solution)/shard_map/ppermute | solution.py:50
  46.3 3.5 %collective-permute-start.9 = (f32[24,512]{1,0:T(8,128)S(1)}, f32[24,512]{1,0:T(8,128)S(1)}, u32[]{:S(2)}, u32[]{:S(2)}) collective-permute-start(f32[24,512]{1,0:T(8,128)S(1)} %add_add_fusion.1), channel_id=1, source_target_pairs={{0,24},{1,25},{2,26},{3,27},{4,28},{5,29},{6,30},{7,31},{8,16},{9,... | collective-permute-start | bytes 147464 | tf_op jit(solution)/shard_map/ppermute | solution.py:58
  50.5 1.9 %collective-permute-done.9 = f32[24,512]{1,0:T(8,128)S(1)} collective-permute-done((f32[24,512]{1,0:T(8,128)S(1)}, f32[24,512]{1,0:T(8,128)S(1)}, u32[]{:S(2)}, u32[]{:S(2)}) %collective-permute-start.9) | collective-permute-done | bytes 49184 | tf_op jit(solution)/shard_map/ppermute | solution.py:58
  56.0 2.2 %collective-permute-done.10 = f32[96,512]{1,0:T(8,128)S(1)} collective-permute-done((f32[96,512]{1,0:T(8,128)S(1)}, f32[96,512]{1,0:T(8,128)S(1)}, u32[]{:S(2)}, u32[]{:S(2)}) %collective-permute-start.10) | collective-permute-done | bytes 196640 | tf_op jit(solution)/shard_map/ppermute | solution.py:58
  58.2 3.5 %collective-permute-done.11 = f32[96,512]{1,0:T(8,128)S(1)} collective-permute-done((f32[96,512]{1,0:T(8,128)S(1)}, f32[96,512]{1,0:T(8,128)S(1)}, u32[]{:S(2)}, u32[]{:S(2)}) %collective-permute-start.11) | collective-permute-done | bytes 196640 | tf_op jit(solution)/shard_map/ppermute | solution.py:58
  62.0 2.3 %collective-permute-done.13 = f32[384,512]{1,0:T(8,128)S(1)} collective-permute-done((f32[384,512]{1,0:T(8,128)S(1)}, f32[384,512]{1,0:T(8,128)S(1)}, u32[]{:S(2)}, u32[]{:S(2)}) %collective-permute-start.13) | collective-permute-done | bytes 786464 | tf_op jit(solution)/shard_map/ppermute | solution.py:58
  65.4 11.7 %custom-call.22 = f32[128,128]{1,0:T(8,128)S(1)} custom-call(f32[128,128]{1,0:T(8,128)S(1)} %slice.149), custom_call_target="Cholesky" | custom-call | tf_op jit(solution)/shard_map/cholesky/custom-call.1 | solution.py:117
  79.0 9.9 %custom-call.15 = f32[1,128,128]{1,2,0:T(8,128)S(1)} custom-call(f32[1,128,128]{2,1,0:T(8,128)S(1)} %get-tuple-element.11), custom_call_target="InvertDiagBlocksLowerTriangular" | custom-call | tf_op jit(solution)/shard_map/triangular_solve | solution.py:118
  90.3 2.0 %fusion.23 = f32[640,384]{1,0:T(8,128)S(1)} fusion(f32[384,512]{1,0:T(8,128)} %get-tuple-element.16, f32[384,512]{1,0:T(8,128)S(1)} %get-tuple-element.15, f32[640,128]{1,0:T(8,128)S(1)} %fusion.24), kind=kOutput, calls=%fused_computation.20 | convolution fusion | flops 377978880 | bytes 3080192 | tf_op jit(solution)/shard_map/dot_general | solution.py:124
  93.3 11.7 %custom-call.23 = f32[128,128]{1,0:T(8,128)S(1)} custom-call(f32[128,128]{1,0:T(8,128)S(1)} %slice.151), custom_call_target="Cholesky" | custom-call | tf_op jit(solution)/shard_map/cholesky/custom-call.1 | solution.py:117
  107.0 9.8 %custom-call.16 = f32[1,128,128]{1,2,0:T(8,128)S(1)} custom-call(f32[1,128,128]{2,1,0:T(8,128)S(1)} %get-tuple-element.9), custom_call_target="InvertDiagBlocksLowerTriangular" | custom-call | tf_op jit(solution)/shard_map/triangular_solve | solution.py:118
  119.7 11.9 %custom-call.24 = f32[128,128]{1,0:T(8,128)S(1)} custom-call(f32[128,128]{1,0:T(8,128)S(1)} %slice.154), custom_call_target="Cholesky" | custom-call | tf_op jit(solution)/shard_map/cholesky/custom-call.1 | solution.py:117
  133.6 9.8 %custom-call.17 = f32[1,128,128]{1,2,0:T(8,128)S(1)} custom-call(f32[1,128,128]{2,1,0:T(8,128)S(1)} %get-tuple-element.7), custom_call_target="InvertDiagBlocksLowerTriangular" | custom-call | tf_op jit(solution)/shard_map/triangular_solve | solution.py:118
  145.5 11.7 %custom-call.25 = f32[128,128]{1,0:T(8,128)S(1)} custom-call(f32[128,128]{1,0:T(8,128)S(1)} %slice.157), custom_call_target="Cholesky" | custom-call | tf_op jit(solution)/shard_map/cholesky/custom-call.1 | solution.py:117
  159.3 9.8 %custom-call.18 = f32[1,128,128]{1,2,0:T(8,128)S(1)} custom-call(f32[1,128,128]{2,1,0:T(8,128)S(1)} %get-tuple-element.5), custom_call_target="InvertDiagBlocksLowerTriangular" | custom-call | tf_op jit(solution)/shard_map/triangular_solve | solution.py:118
  (84 shorter events, 38.2 us)
Async XLA Ops:
  0.6 10.1 %copy-start = (bf16[4096,256]{1,0:T(8,128)(2,1)S(1)}, bf16[4096,256]{1,0:T(8,128)(2,1)}, u32[]{:S(2)}) copy-start(bf16[4096,256]{1,0:T(8,128)(2,1)} %param.8) | copy-start | bytes 6291460
  4.3 6.4 %copy-start.4 = (bf16[4096,512]{1,0:T(8,128)(2,1)S(1)}, bf16[4096,512]{1,0:T(8,128)(2,1)}, u32[]{:S(2)}) copy-start(bf16[4096,512]{1,0:T(8,128)(2,1)} %param.7) | copy-start | bytes 12582916
  15.4 2.7 %collective-permute-start = (f32[384,512]{1,0:T(8,128)}, f32[384,512]{1,0:T(8,128)}, u32[]{:S(2)}, u32[]{:S(2)}) collective-permute-start(f32[384,512]{1,0:T(8,128)} %slice_select_fusion), channel_id=1, source_target_pairs={{0,1},{1,0},{2,3},{3,2},{4,5},{5,4},{6,7},{7,6},{8,9},{9,8},{10,11... | collective-permute-start | bytes 2359304 | tf_op jit(solution)/shard_map/ppermute | solution.py:50
  19.7 4.6 %copy-start.1 = (f32[384,512]{1,0:T(8,128)}, f32[384,512]{1,0:T(8,128)S(1)}, u32[]{:S(2)}) copy-start(f32[384,512]{1,0:T(8,128)S(1)} %select_add_fusion) | copy-start | bytes 2359300
  19.7 8.6 %collective-permute-start.1 = (f32[96,512]{1,0:T(8,128)S(1)}, f32[96,512]{1,0:T(8,128)S(1)}, u32[]{:S(2)}, u32[]{:S(2)}) collective-permute-start(f32[96,512]{1,0:T(8,128)S(1)} %get-tuple-element.21), channel_id=1, source_target_pairs={{0,2},{1,3},{2,0},{3,1},{4,6},{5,7},{6,4},{7,5},{8,10},{9,11},{10,... | collective-permute-start | bytes 589832 | tf_op jit(solution)/shard_map/ppermute | solution.py:50
  22.7 10.9 %collective-permute-start.2 = (f32[96,512]{1,0:T(8,128)S(1)}, f32[96,512]{1,0:T(8,128)S(1)}, u32[]{:S(2)}, u32[]{:S(2)}) collective-permute-start(f32[96,512]{1,0:T(8,128)S(1)} %get-tuple-element.22), channel_id=1, source_target_pairs={{0,4},{1,5},{2,6},{3,7},{4,0},{5,1},{6,2},{7,3},{8,12},{9,13},{10,... | collective-permute-start | bytes 589832 | tf_op jit(solution)/shard_map/ppermute | solution.py:50
  24.3 9.3 %collective-permute-start.3 = (f32[96,512]{1,0:T(8,128)S(1)}, f32[96,512]{1,0:T(8,128)S(1)}, u32[]{:S(2)}, u32[]{:S(2)}) collective-permute-start(f32[96,512]{1,0:T(8,128)S(1)} %select_select_fusion.4), channel_id=1, source_target_pairs={{0,6},{1,7},{2,4},{3,5},{4,2},{5,3},{6,0},{7,1},{8,14},{9,15},{10,... | collective-permute-start | bytes 589832 | tf_op jit(solution)/shard_map/ppermute | solution.py:50
  34.9 4.6 %collective-permute-start.4 = (f32[24,512]{1,0:T(8,128)S(1)}, f32[24,512]{1,0:T(8,128)S(1)}, u32[]{:S(2)}, u32[]{:S(2)}) collective-permute-start(f32[24,512]{1,0:T(8,128)S(1)} %get-tuple-element.27), channel_id=1, source_target_pairs={{0,8},{1,9},{2,10},{3,11},{4,12},{5,13},{6,14},{7,15},{8,0},{9,1},... | collective-permute-start | bytes 147464 | tf_op jit(solution)/shard_map/ppermute | solution.py:50
  36.6 5.5 %collective-permute-start.5 = (f32[24,512]{1,0:T(8,128)S(1)}, f32[24,512]{1,0:T(8,128)S(1)}, u32[]{:S(2)}, u32[]{:S(2)}) collective-permute-start(f32[24,512]{1,0:T(8,128)S(1)} %get-tuple-element.28), channel_id=1, source_target_pairs={{0,16},{1,17},{2,18},{3,19},{4,20},{5,21},{6,22},{7,23},{8,24},{9,... | collective-permute-start | bytes 147464 | tf_op jit(solution)/shard_map/ppermute | solution.py:50
  39.2 6.2 %collective-permute-start.6 = (f32[24,512]{1,0:T(8,128)S(1)}, f32[24,512]{1,0:T(8,128)S(1)}, u32[]{:S(2)}, u32[]{:S(2)}) collective-permute-start(f32[24,512]{1,0:T(8,128)S(1)} %select_select_fusion.15), channel_id=1, source_target_pairs={{0,24},{1,25},{2,26},{3,27},{4,28},{5,29},{6,30},{7,31},{8,16},{9,... | collective-permute-start | bytes 147464 | tf_op jit(solution)/shard_map/ppermute | solution.py:50
  45.4 4.5 %collective-permute-start.7 = (f32[24,512]{1,0:T(8,128)S(1)}, f32[24,512]{1,0:T(8,128)S(1)}, u32[]{:S(2)}, u32[]{:S(2)}) collective-permute-start(f32[24,512]{1,0:T(8,128)S(1)} %add_add_fusion.1), channel_id=1, source_target_pairs={{0,8},{1,9},{2,10},{3,11},{4,12},{5,13},{6,14},{7,15},{8,0},{9,1},... | collective-permute-start | bytes 147464 | tf_op jit(solution)/shard_map/ppermute | solution.py:58
  45.5 5.1 %collective-permute-start.8 = (f32[24,512]{1,0:T(8,128)S(1)}, f32[24,512]{1,0:T(8,128)S(1)}, u32[]{:S(2)}, u32[]{:S(2)}) collective-permute-start(f32[24,512]{1,0:T(8,128)S(1)} %add_add_fusion.1), channel_id=1, source_target_pairs={{0,16},{1,17},{2,18},{3,19},{4,20},{5,21},{6,22},{7,23},{8,24},{9,... | collective-permute-start | bytes 147464 | tf_op jit(solution)/shard_map/ppermute | solution.py:58
  46.3 6.1 %collective-permute-start.9 = (f32[24,512]{1,0:T(8,128)S(1)}, f32[24,512]{1,0:T(8,128)S(1)}, u32[]{:S(2)}, u32[]{:S(2)}) collective-permute-start(f32[24,512]{1,0:T(8,128)S(1)} %add_add_fusion.1), channel_id=1, source_target_pairs={{0,24},{1,25},{2,26},{3,27},{4,28},{5,29},{6,30},{7,31},{8,16},{9,... | collective-permute-start | bytes 147464 | tf_op jit(solution)/shard_map/ppermute | solution.py:58
  52.5 5.7 %collective-permute-start.10 = (f32[96,512]{1,0:T(8,128)S(1)}, f32[96,512]{1,0:T(8,128)S(1)}, u32[]{:S(2)}, u32[]{:S(2)}) collective-permute-start(f32[96,512]{1,0:T(8,128)S(1)} %pad_maximum_fusion.4), channel_id=1, source_target_pairs={{0,2},{1,3},{2,0},{3,1},{4,6},{5,7},{6,4},{7,5},{8,10},{9,11},{10,... | collective-permute-start | bytes 589832 | tf_op jit(solution)/shard_map/ppermute | solution.py:58
  54.0 7.8 %collective-permute-start.11 = (f32[96,512]{1,0:T(8,128)S(1)}, f32[96,512]{1,0:T(8,128)S(1)}, u32[]{:S(2)}, u32[]{:S(2)}) collective-permute-start(f32[96,512]{1,0:T(8,128)S(1)} %pad_maximum_fusion.4), channel_id=1, source_target_pairs={{0,4},{1,5},{2,6},{3,7},{4,0},{5,1},{6,2},{7,3},{8,12},{9,13},{10,... | collective-permute-start | bytes 589832 | tf_op jit(solution)/shard_map/ppermute | solution.py:58
  54.6 7.1 %collective-permute-start.12 = (f32[96,512]{1,0:T(8,128)S(1)}, f32[96,512]{1,0:T(8,128)S(1)}, u32[]{:S(2)}, u32[]{:S(2)}) collective-permute-start(f32[96,512]{1,0:T(8,128)S(1)} %pad_maximum_fusion.4), channel_id=1, source_target_pairs={{0,6},{1,7},{2,4},{3,5},{4,2},{5,3},{6,0},{7,1},{8,14},{9,15},{10,... | collective-permute-start | bytes 589832 | tf_op jit(solution)/shard_map/ppermute | solution.py:58
  61.9 2.4 %collective-permute-start.13 = (f32[384,512]{1,0:T(8,128)S(1)}, f32[384,512]{1,0:T(8,128)S(1)}, u32[]{:S(2)}, u32[]{:S(2)}) collective-permute-start(f32[384,512]{1,0:T(8,128)S(1)} %pad_maximum_fusion.3), channel_id=1, source_target_pairs={{0,1},{1,0},{2,3},{3,2},{4,5},{5,4},{6,7},{7,6},{8,9},{9,8},{10,11... | collective-permute-start | bytes 2359304 | tf_op jit(solution)/shard_map/ppermute | solution.py:58
  92.3 0.9 copy-start.2
  144.1 1.4 copy-start.3
where the time goes:
time: 176 us; the launch traced here: 175 us
  other arithmetic  105 us (60%)
  waiting for transfers between devices  27.8 us (16%)
  starting transfers between devices  17.7 us (10%)
  matrix products  17.5 us (10%)
  local copies, waits for them, and re-layouts  5.37 us (3%)
    another operation x12, other arithmetic, factor_and_solve(): diag = lax.linalg.cholesky(trail[:block, :block], symmetrize_input=False)  49.8 us
    another operation x8, other arithmetic, factor_and_solve(): lax.linalg.triangular_solve(diag, trail[block:, :block], left_side=False,...  44.5 us
    ppermute x7, waiting for transfers between devices, exchange_sum(): acc = acc + lax.ppermute(pick(parts, digit ^ a), AXES, pairs)  17.2 us
    ppermute x7, waiting for transfers between devices, exchange_sum(): got.append(lax.ppermute(cur, AXES, pairs))  10.6 us
    ppermute x7, starting transfers between devices, exchange_sum(): acc = acc + lax.ppermute(pick(parts, digit ^ a), AXES, pairs)  9.64 us
    dot_general x2, matrix products, contract(): lax.dot_general(left, right, (((0,), (0,)), ((), ())), precision=precisio...  9.04 us
    ppermute x7, starting transfers between devices, exchange_sum(): got.append(lax.ppermute(cur, AXES, pairs))  8.07 us
    another operation x4, matrix products, factor_and_solve(): lax.linalg.triangular_solve(diag, trail[block:, :block], left_side=False,...  4.13 us
  transfers between devices with their start and end apart: 14, of which 11 were waited for; matrix products, arithmetic and copies ran while one was open for 0% of the time, Pallas kernels for 0%

commit v1 on v0

--- a/solution.py
+++ b/solution.py
@@ -114,11 +114,11 @@
     n = trail.shape[1]
     columns = []
     for s in range(0, n, block):
-        diag = lax.linalg.cholesky(trail[:block, :block], symmetrize_input=False)
+        diag = lax.linalg.cholesky_p.bind(trail[:block, :block])
         panel = lax.linalg.triangular_solve(
             diag, trail[block:, :block], left_side=False, lower=True, transpose_a=True
         )
-        columns.append(jnp.concatenate([diag, panel], axis=0))
+        columns.append(jnp.concatenate([jnp.tril(diag), panel], axis=0))
         if s + block < n:
             upper = panel[: n - s - block]
             trail = trail[block:, block:] - lax.dot_general(

time: 176 us -> 181 us (1.028)
  other arithmetic: 105 us -> 108 us
    select_n x0 -> x4, other arithmetic: none -> 5.14 us  [factor_and_solve(): columns.append(jnp.concatenate([jnp.tril(diag), panel], axis=0))]
    another operation x8, other arithmetic: 44.5 us -> 42.4 us  [factor_and_solve(): lax.linalg.triangular_solve(diag, trail[block:, :block], left_side=False,...]
where the time goes in v1:
time: 181 us; the launch traced here: 180 us
  other arithmetic  108 us (60%)
  waiting for transfers between devices  27.8 us (15%)
  matrix products  18.4 us (10%)
  starting transfers between devices  17.7 us (10%)
  local copies, waits for them, and re-layouts  6.03 us (3%)
    another operation x12, other arithmetic, factor_and_solve(): diag = lax.linalg.cholesky_p.bind(trail[:block, :block])  49.8 us
    another operation x8, other arithmetic, factor_and_solve(): lax.linalg.triangular_solve(diag, trail[block:, :block], left_side=False,...  42.4 us
    ppermute x7, waiting for transfers between devices, exchange_sum(): acc = acc + lax.ppermute(pick(parts, digit ^ a), AXES, pairs)  17.2 us
    ppermute x7, waiting for transfers between devices, exchange_sum(): got.append(lax.ppermute(cur, AXES, pairs))  10.6 us
    ppermute x7, starting transfers between devices, exchange_sum(): acc = acc + lax.ppermute(pick(parts, digit ^ a), AXES, pairs)  9.64 us
    dot_general x2, matrix products, contract(): lax.dot_general(left, right, (((0,), (0,)), ((), ())), precision=precisio...  9.04 us
    ppermute x7, starting transfers between devices, exchange_sum(): got.append(lax.ppermute(cur, AXES, pairs))  8.07 us
    select_n x4, other arithmetic, factor_and_solve(): columns.append(jnp.concatenate([jnp.tril(diag), panel], axis=0))  5.14 us
  transfers between devices with their start and end apart: 14, of which 11 were waited for; matrix products, arithmetic and copies ran while one was open for 0% of the time, Pallas kernels for 0%

profile of v1, /device:TPU:0, one launch (start us, length us, event | category | flops | bytes accessed | tf_op | source)
XLA Modules:
  0.0 180.0 jit_solution(5376128478995776612)
XLA Ops:
  4.3 6.4 %fusion.11 = f32[512,512]{1,0:T(8,128)S(1)} fusion(bf16[4096,512]{1,0:T(8,128)(2,1)} %param.7, pred[4096]{0:T(1024)(128)(4,1)S(1)} %fusion.61, f32[512,768]{0,1:T(8,128)S(1)} %fusion.65), kind=kOutput, calls=%fused_computation.9 | convolution fusion | flops 2149842944 | bytes 10489856 | tf_op jit(solution)/shard_map/dot_general | solution.py:11
  10.8 2.6 %fusion.17 = f32[256,512]{1,0:T(8,128)} fusion(bf16[4096,256]{1,0:T(8,128)(2,1)S(1)} %copy-done, bf16[4096,512]{1,0:T(8,128)(2,1)S(1)} %copy-done.5, pred[4096]{0:T(1024)(128)(4,1)S(1)} %fusion.61, f32[512,768]{0,1:T(8,128)S(1)} %fusion.65), kind=kOutput, calls=%fused_computation.11 | convolution fusion | flops 1075970048 | bytes 7344128 | tf_op jit(solution)/shard_map/dot_general | solution.py:11
  13.4 2.1 %slice_select_fusion = f32[384,512]{1,0:T(8,128)} fusion(f32[512,512]{1,0:T(8,128)S(1)} %fusion.11, pred[]{:T(512)S(6)} %eq.115, f32[256,512]{1,0:T(8,128)} %fusion.17), kind=kLoop, calls=%fused_computation.24 | loop fusion | flops 393216 | bytes 3145729 | tf_op jit(solution)/shard_map/jit(_where)/select_n | solution.py:34
  15.9 2.3 %collective-permute-done = f32[384,512]{1,0:T(8,128)} collective-permute-done((f32[384,512]{1,0:T(8,128)}, f32[384,512]{1,0:T(8,128)}, u32[]{:S(2)}, u32[]{:S(2)}) %collective-permute-start) | collective-permute-done | bytes 786464 | tf_op jit(solution)/shard_map/ppermute | solution.py:50
  19.7 2.9 %collective-permute-start.1 = (f32[96,512]{1,0:T(8,128)S(1)}, f32[96,512]{1,0:T(8,128)S(1)}, u32[]{:S(2)}, u32[]{:S(2)}) collective-permute-start(f32[96,512]{1,0:T(8,128)S(1)} %get-tuple-element.13), channel_id=1, source_target_pairs={{0,2},{1,3},{2,0},{3,1},{4,6},{5,7},{6,4},{7,5},{8,10},{9,11},{10,... | collective-permute-start | bytes 589832 | tf_op jit(solution)/shard_map/ppermute | solution.py:50
  24.5 3.9 %collective-permute-done.1 = f32[96,512]{1,0:T(8,128)S(1)} collective-permute-done((f32[96,512]{1,0:T(8,128)S(1)}, f32[96,512]{1,0:T(8,128)S(1)}, u32[]{:S(2)}, u32[]{:S(2)}) %collective-permute-start.1) | collective-permute-done | bytes 196640 | tf_op jit(solution)/shard_map/ppermute | solution.py:50
  28.4 5.2 %collective-permute-done.2 = f32[96,512]{1,0:T(8,128)S(1)} collective-permute-done((f32[96,512]{1,0:T(8,128)S(1)}, f32[96,512]{1,0:T(8,128)S(1)}, u32[]{:S(2)}, u32[]{:S(2)}) %collective-permute-start.2) | collective-permute-done | bytes 196640 | tf_op jit(solution)/shard_map/ppermute | solution.py:50
  36.6 2.6 %collective-permute-start.5 = (f32[24,512]{1,0:T(8,128)S(1)}, f32[24,512]{1,0:T(8,128)S(1)}, u32[]{:S(2)}, u32[]{:S(2)}) collective-permute-start(f32[24,512]{1,0:T(8,128)S(1)} %get-tuple-element.20), channel_id=1, source_target_pairs={{0,16},{1,17},{2,18},{3,19},{4,20},{5,21},{6,22},{7,23},{8,24},{9,... | collective-permute-start | bytes 147464 | tf_op jit(solution)/shard_map/ppermute | solution.py:50
  39.5 2.6 %collective-permute-done.5 = f32[24,512]{1,0:T(8,128)S(1)} collective-permute-done((f32[24,512]{1,0:T(8,128)S(1)}, f32[24,512]{1,0:T(8,128)S(1)}, u32[]{:S(2)}, u32[]{:S(2)}) %collective-permute-start.5) | collective-permute-done | bytes 49184 | tf_op jit(solution)/shard_map/ppermute | solution.py:50
  42.1 3.3 %collective-permute-done.6 = f32[24,512]{1,0:T(8,128)S(1)} collective-permute-done((f32[24,512]{1,0:T(8,128)S(1)}, f32[24,512]{1,0:T(8,128)S(1)}, u32[]{:S(2)}, u32[]{:S(2)}) %collective-permute-start.6) | collective-permute-done | bytes 49184 | tf_op jit(solution)/shard_map/ppermute | solution.py:50
  46.3 3.5 %collective-permute-start.9 = (f32[24,512]{1,0:T(8,128)S(1)}, f32[24,512]{1,0:T(8,128)S(1)}, u32[]{:S(2)}, u32[]{:S(2)}) collective-permute-start(f32[24,512]{1,0:T(8,128)S(1)} %add_add_fusion.1), channel_id=1, source_target_pairs={{0,24},{1,25},{2,26},{3,27},{4,28},{5,29},{6,30},{7,31},{8,16},{9,... | collective-permute-start | bytes 147464 | tf_op jit(solution)/shard_map/ppermute | solution.py:58
  56.0 2.2 %collective-permute-done.10 = f32[96,512]{1,0:T(8,128)S(1)} collective-permute-done((f32[96,512]{1,0:T(8,128)S(1)}, f32[96,512]{1,0:T(8,128)S(1)}, u32[]{:S(2)}, u32[]{:S(2)}) %collective-permute-start.10) | collective-permute-done | bytes 196640 | tf_op jit(solution)/shard_map/ppermute | solution.py:58
  58.2 3.5 %collective-permute-done.11 = f32[96,512]{1,0:T(8,128)S(1)} collective-permute-done((f32[96,512]{1,0:T(8,128)S(1)}, f32[96,512]{1,0:T(8,128)S(1)}, u32[]{:S(2)}, u32[]{:S(2)}) %collective-permute-start.11) | collective-permute-done | bytes 196640 | tf_op jit(solution)/shard_map/ppermute | solution.py:58
  62.0 2.3 %collective-permute-done.13 = f32[384,512]{1,0:T(8,128)S(1)} collective-permute-done((f32[384,512]{1,0:T(8,128)S(1)}, f32[384,512]{1,0:T(8,128)S(1)}, u32[]{:S(2)}, u32[]{:S(2)}) %collective-permute-start.13) | collective-permute-done | bytes 786464 | tf_op jit(solution)/shard_map/ppermute | solution.py:58
  65.4 11.7 %custom-call.22 = f32[128,128]{1,0:T(8,128)S(1)} custom-call(f32[128,128]{1,0:T(8,128)S(1)} %slice.149), custom_call_target="Cholesky" | custom-call | tf_op jit(solution)/shard_map/cholesky/custom-call.1 | solution.py:117
  78.3 9.9 %custom-call.15 = f32[1,128,128]{1,2,0:T(8,128)S(1)} custom-call(f32[1,128,128]{2,1,0:T(8,128)S(1)} %fusion.76), custom_call_target="InvertDiagBlocksLowerTriangular" | custom-call | tf_op jit(solution)/shard_map/triangular_solve | solution.py:118
  89.6 2.0 %fusion.23 = f32[640,384]{1,0:T(8,128)S(1)} fusion(f32[384,512]{1,0:T(8,128)} %get-tuple-element.8, f32[384,512]{1,0:T(8,128)S(1)} %get-tuple-element.7, f32[640,128]{1,0:T(8,128)S(1)} %fusion.24), kind=kOutput, calls=%fused_computation.20 | convolution fusion | flops 377978880 | bytes 3080192 | tf_op jit(solution)/shard_map/dot_general | solution.py:124
  92.6 11.7 %custom-call.23 = f32[128,128]{1,0:T(8,128)S(1)} custom-call(f32[128,128]{1,0:T(8,128)S(1)} %slice.151), custom_call_target="Cholesky" | custom-call | tf_op jit(solution)/shard_map/cholesky/custom-call.1 | solution.py:117
  105.6 9.8 %custom-call.16 = f32[1,128,128]{1,2,0:T(8,128)S(1)} custom-call(f32[1,128,128]{2,1,0:T(8,128)S(1)} %fusion.75), custom_call_target="InvertDiagBlocksLowerTriangular" | custom-call | tf_op jit(solution)/shard_map/triangular_solve | solution.py:118
  118.4 11.9 %custom-call.24 = f32[128,128]{1,0:T(8,128)S(1)} custom-call(f32[128,128]{1,0:T(8,128)S(1)} %slice.154), custom_call_target="Cholesky" | custom-call | tf_op jit(solution)/shard_map/cholesky/custom-call.1 | solution.py:117
  131.7 10.4 %custom-call.17 = f32[1,128,128]{1,2,0:T(8,128)} custom-call(f32[1,128,128]{2,1,0:T(8,128)S(1)} %fusion.74), custom_call_target="InvertDiagBlocksLowerTriangular" | custom-call | tf_op jit(solution)/shard_map/triangular_solve | solution.py:118
  146.9 2.1 %select_select_fusion.8 = f32[128,128]{1,0:T(8,128)} fusion(f32[128,128]{1,0:T(8,128)} %copy-done.4, pred[]{:T(512)} %compare_reduce_fusion.1), kind=kLoop, calls=%fused_computation.65 | loop fusion | flops 49152 | bytes 131073 | tf_op jit(solution)/shard_map/jit(tril)/select_n | solution.py:121
  149.6 11.7 %custom-call.25 = f32[128,128]{1,0:T(8,128)S(1)} custom-call(f32[128,128]{1,0:T(8,128)S(1)} %slice.157), custom_call_target="Cholesky" | custom-call | tf_op jit(solution)/shard_map/cholesky/custom-call.1 | solution.py:117
  163.8 9.8 %custom-call.18 = f32[1,128,128]{1,2,0:T(8,128)S(1)} custom-call(f32[1,128,128]{2,1,0:T(8,128)S(1)} %fusion.73), custom_call_target="InvertDiagBlocksLowerTriangular" | custom-call | tf_op jit(solution)/shard_map/triangular_solve | solution.py:118
  (90 shorter events, 42.0 us)
Async XLA Ops:
  0.6 10.1 %copy-start = (bf16[4096,256]{1,0:T(8,128)(2,1)S(1)}, bf16[4096,256]{1,0:T(8,128)(2,1)}, u32[]{:S(2)}) copy-start(bf16[4096,256]{1,0:T(8,128)(2,1)} %param.8) | copy-start | bytes 6291460
  4.3 6.4 %copy-start.5 = (bf16[4096,512]{1,0:T(8,128)(2,1)S(1)}, bf16[4096,512]{1,0:T(8,128)(2,1)}, u32[]{:S(2)}) copy-start(bf16[4096,512]{1,0:T(8,128)(2,1)} %param.7) | copy-start | bytes 12582916
  15.4 2.7 %collective-permute-start = (f32[384,512]{1,0:T(8,128)}, f32[384,512]{1,0:T(8,128)}, u32[]{:S(2)}, u32[]{:S(2)}) collective-permute-start(f32[384,512]{1,0:T(8,128)} %slice_select_fusion), channel_id=1, source_target_pairs={{0,1},{1,0},{2,3},{3,2},{4,5},{5,4},{6,7},{7,6},{8,9},{9,8},{10,11... | collective-permute-start | bytes 2359304 | tf_op jit(solution)/shard_map/ppermute | solution.py:50
  19.7 4.6 %copy-start.1 = (f32[384,512]{1,0:T(8,128)}, f32[384,512]{1,0:T(8,128)S(1)}, u32[]{:S(2)}) copy-start(f32[384,512]{1,0:T(8,128)S(1)} %select_add_fusion) | copy-start | bytes 2359300
  19.7 8.6 %collective-permute-start.1 = (f32[96,512]{1,0:T(8,128)S(1)}, f32[96,512]{1,0:T(8,128)S(1)}, u32[]{:S(2)}, u32[]{:S(2)}) collective-permute-start(f32[96,512]{1,0:T(8,128)S(1)} %get-tuple-element.13), channel_id=1, source_target_pairs={{0,2},{1,3},{2,0},{3,1},{4,6},{5,7},{6,4},{7,5},{8,10},{9,11},{10,... | collective-permute-start | bytes 589832 | tf_op jit(solution)/shard_map/ppermute | solution.py:50
  22.7 10.9 %collective-permute-start.2 = (f32[96,512]{1,0:T(8,128)S(1)}, f32[96,512]{1,0:T(8,128)S(1)}, u32[]{:S(2)}, u32[]{:S(2)}) collective-permute-start(f32[96,512]{1,0:T(8,128)S(1)} %get-tuple-element.14), channel_id=1, source_target_pairs={{0,4},{1,5},{2,6},{3,7},{4,0},{5,1},{6,2},{7,3},{8,12},{9,13},{10,... | collective-permute-start | bytes 589832 | tf_op jit(solution)/shard_map/ppermute | solution.py:50
  24.3 9.3 %collective-permute-start.3 = (f32[96,512]{1,0:T(8,128)S(1)}, f32[96,512]{1,0:T(8,128)S(1)}, u32[]{:S(2)}, u32[]{:S(2)}) collective-permute-start(f32[96,512]{1,0:T(8,128)S(1)} %select_select_fusion.4), channel_id=1, source_target_pairs={{0,6},{1,7},{2,4},{3,5},{4,2},{5,3},{6,0},{7,1},{8,14},{9,15},{10,... | collective-permute-start | bytes 589832 | tf_op jit(solution)/shard_map/ppermute | solution.py:50
  34.9 4.6 %collective-permute-start.4 = (f32[24,512]{1,0:T(8,128)S(1)}, f32[24,512]{1,0:T(8,128)S(1)}, u32[]{:S(2)}, u32[]{:S(2)}) collective-permute-start(f32[24,512]{1,0:T(8,128)S(1)} %get-tuple-element.19), channel_id=1, source_target_pairs={{0,8},{1,9},{2,10},{3,11},{4,12},{5,13},{6,14},{7,15},{8,0},{9,1},... | collective-permute-start | bytes 147464 | tf_op jit(solution)/shard_map/ppermute | solution.py:50
  36.6 5.5 %collective-permute-start.5 = (f32[24,512]{1,0:T(8,128)S(1)}, f32[24,512]{1,0:T(8,128)S(1)}, u32[]{:S(2)}, u32[]{:S(2)}) collective-permute-start(f32[24,512]{1,0:T(8,128)S(1)} %get-tuple-element.20), channel_id=1, source_target_pairs={{0,16},{1,17},{2,18},{3,19},{4,20},{5,21},{6,22},{7,23},{8,24},{9,... | collective-permute-start | bytes 147464 | tf_op jit(solution)/shard_map/ppermute | solution.py:50
  39.2 6.2 %collective-permute-start.6 = (f32[24,512]{1,0:T(8,128)S(1)}, f32[24,512]{1,0:T(8,128)S(1)}, u32[]{:S(2)}, u32[]{:S(2)}) collective-permute-start(f32[24,512]{1,0:T(8,128)S(1)} %select_select_fusion.15), channel_id=1, source_target_pairs={{0,24},{1,25},{2,26},{3,27},{4,28},{5,29},{6,30},{7,31},{8,16},{9,... | collective-permute-start | bytes 147464 | tf_op jit(solution)/shard_map/ppermute | solution.py:50
  45.4 4.5 %collective-permute-start.7 = (f32[24,512]{1,0:T(8,128)S(1)}, f32[24,512]{1,0:T(8,128)S(1)}, u32[]{:S(2)}, u32[]{:S(2)}) collective-permute-start(f32[24,512]{1,0:T(8,128)S(1)} %add_add_fusion.1), channel_id=1, source_target_pairs={{0,8},{1,9},{2,10},{3,11},{4,12},{5,13},{6,14},{7,15},{8,0},{9,1},... | collective-permute-start | bytes 147464 | tf_op jit(solution)/shard_map/ppermute | solution.py:58
  45.5 5.1 %collective-permute-start.8 = (f32[24,512]{1,0:T(8,128)S(1)}, f32[24,512]{1,0:T(8,128)S(1)}, u32[]{:S(2)}, u32[]{:S(2)}) collective-permute-start(f32[24,512]{1,0:T(8,128)S(1)} %add_add_fusion.1), channel_id=1, source_target_pairs={{0,16},{1,17},{2,18},{3,19},{4,20},{5,21},{6,22},{7,23},{8,24},{9,... | collective-permute-start | bytes 147464 | tf_op jit(solution)/shard_map/ppermute | solution.py:58
  46.3 6.1 %collective-permute-start.9 = (f32[24,512]{1,0:T(8,128)S(1)}, f32[24,512]{1,0:T(8,128)S(1)}, u32[]{:S(2)}, u32[]{:S(2)}) collective-permute-start(f32[24,512]{1,0:T(8,128)S(1)} %add_add_fusion.1), channel_id=1, source_target_pairs={{0,24},{1,25},{2,26},{3,27},{4,28},{5,29},{6,30},{7,31},{8,16},{9,... | collective-permute-start | bytes 147464 | tf_op jit(solution)/shard_map/ppermute | solution.py:58
  52.5 5.7 %collective-permute-start.10 = (f32[96,512]{1,0:T(8,128)S(1)}, f32[96,512]{1,0:T(8,128)S(1)}, u32[]{:S(2)}, u32[]{:S(2)}) collective-permute-start(f32[96,512]{1,0:T(8,128)S(1)} %pad_maximum_fusion.4), channel_id=1, source_target_pairs={{0,2},{1,3},{2,0},{3,1},{4,6},{5,7},{6,4},{7,5},{8,10},{9,11},{10,... | collective-permute-start | bytes 589832 | tf_op jit(solution)/shard_map/ppermute | solution.py:58
  54.0 7.8 %collective-permute-start.11 = (f32[96,512]{1,0:T(8,128)S(1)}, f32[96,512]{1,0:T(8,128)S(1)}, u32[]{:S(2)}, u32[]{:S(2)}) collective-permute-start(f32[96,512]{1,0:T(8,128)S(1)} %pad_maximum_fusion.4), channel_id=1, source_target_pairs={{0,4},{1,5},{2,6},{3,7},{4,0},{5,1},{6,2},{7,3},{8,12},{9,13},{10,... | collective-permute-start | bytes 589832 | tf_op jit(solution)/shard_map/ppermute | solution.py:58
  54.6 7.1 %collective-permute-start.12 = (f32[96,512]{1,0:T(8,128)S(1)}, f32[96,512]{1,0:T(8,128)S(1)}, u32[]{:S(2)}, u32[]{:S(2)}) collective-permute-start(f32[96,512]{1,0:T(8,128)S(1)} %pad_maximum_fusion.4), channel_id=1, source_target_pairs={{0,6},{1,7},{2,4},{3,5},{4,2},{5,3},{6,0},{7,1},{8,14},{9,15},{10,... | collective-permute-start | bytes 589832 | tf_op jit(solution)/shard_map/ppermute | solution.py:58
  61.9 2.4 %collective-permute-start.13 = (f32[384,512]{1,0:T(8,128)S(1)}, f32[384,512]{1,0:T(8,128)S(1)}, u32[]{:S(2)}, u32[]{:S(2)}) collective-permute-start(f32[384,512]{1,0:T(8,128)S(1)} %pad_maximum_fusion.3), channel_id=1, source_target_pairs={{0,1},{1,0},{2,3},{3,2},{4,5},{5,4},{6,7},{7,6},{8,9},{9,8},{10,11... | collective-permute-start | bytes 2359304 | tf_op jit(solution)/shard_map/ppermute | solution.py:58
  91.6 0.9 copy-start.2
  130.3 1.4 copy-start.4
  143.6 6.0 %copy-start.3 = (f32[384,128]{1,0:T(8,128)}, f32[384,128]{1,0:T(8,128)S(1)}, u32[]{:S(2)}) copy-start(f32[384,128]{1,0:T(8,128)S(1)} %convolution_subtract_fusion) | copy-start | bytes 589828

commit v2 on v0

--- a/solution.py
+++ b/solution.py
@@ -43,11 +43,11 @@
         radix = 1 << width
         digit = (idx >> k) & (radix - 1)
         size = cur.shape[0] // radix
-        parts = [cur[t * size : (t + 1) * size] for t in range(radix)]
-        acc = pick(parts, digit)
+        acc = lax.dynamic_slice_in_dim(cur, digit * size, size, 0)
         for a in range(1, radix):
             pairs = [(i, i ^ (a << k)) for i in range(n_dev)]
-            acc = acc + lax.ppermute(pick(parts, digit ^ a), AXES, pairs)
+            sent = lax.dynamic_slice_in_dim(cur, (digit ^ a) * size, size, 0)
+            acc = acc + lax.ppermute(sent, AXES, pairs)
         cur = acc
     for k, width in reversed(groups):
         radix = 1 << width

time: 176 us -> 179 us (1.017)
  other arithmetic: 105 us -> 107 us
    concatenate x0 -> x1, other arithmetic: none -> 2.11 us  [body(): both = summed(jnp.concatenate([gram.T, cross.T], axis=0), n_dev)]
    unnamed x12 -> x24, local copies, waits for them, and re-layouts: 3.27 us -> 4.84 us
  transfers between devices with their start and end apart: 14 -> 14, of which waited for: 11 -> 10; matrix products, arithmetic and copies ran while one was open for 0% -> 0% of each run, Pallas kernels for 0% -> 0%
where the time goes in v2:
time: 179 us; the launch traced here: 178 us
  other arithmetic  107 us (60%)
  waiting for transfers between devices  28.9 us (16%)
  starting transfers between devices  17 us (9%)
  matrix products  16.5 us (9%)
  local copies, waits for them, and re-layouts  7.01 us (4%)
    another operation x12, other arithmetic, factor_and_solve(): diag = lax.linalg.cholesky(trail[:block, :block], symmetrize_input=False)  49.8 us
    another operation x8, other arithmetic, factor_and_solve(): lax.linalg.triangular_solve(diag, trail[block:, :block], left_side=False,...  44.5 us
    ppermute x7, waiting for transfers between devices, exchange_sum(): acc = acc + lax.ppermute(sent, AXES, pairs)  18.3 us
    ppermute x7, waiting for transfers between devices, exchange_sum(): got.append(lax.ppermute(cur, AXES, pairs))  10.7 us
    dot_general x2, matrix products, contract(): lax.dot_general(left, right, (((0,), (0,)), ((), ())), precision=precisio...  9.03 us
    ppermute x7, starting transfers between devices, exchange_sum(): acc = acc + lax.ppermute(sent, AXES, pairs)  9 us
    ppermute x7, starting transfers between devices, exchange_sum(): got.append(lax.ppermute(cur, AXES, pairs))  8 us
    unnamed x24, local copies, waits for them, and re-layouts  4.84 us
  transfers between devices with their start and end apart: 14, of which 10 were waited for; matrix products, arithmetic and copies ran while one was open for 0% of the time, Pallas kernels for 0%

profile of v2, /device:TPU:0, one launch (start us, length us, event | category | flops | bytes accessed | tf_op | source)
XLA Modules:
  0.0 178.2 jit_solution(11696243792222034455)
XLA Ops:
  3.6 6.4 %fusion.11 = f32[512,512]{1,0:T(8,128)S(1)} fusion(bf16[4096,512]{1,0:T(8,128)(2,1)} %param.7, pred[4096]{0:T(1024)(128)(4,1)S(1)} %fusion.64, f32[512,768]{0,1:T(8,128)S(1)} %fusion.68), kind=kOutput, calls=%fused_computation.13 | convolution fusion | flops 2149842944 | bytes 10489856 | tf_op jit(solution)/shard_map/dot_general | solution.py:11
  10.1 2.6 %fusion.17 = f32[256,512]{1,0:T(8,128)} fusion(bf16[4096,256]{1,0:T(8,128)(2,1)S(1)} %copy-done, bf16[4096,512]{1,0:T(8,128)(2,1)S(1)} %copy-done.10, pred[4096]{0:T(1024)(128)(4,1)S(1)} %fusion.64, f32[512,768]{0,1:T(8,128)S(1)} %fusion.68), kind=kOutput, calls=%fused_computation.15 | convolution fusion | flops 1075970048 | bytes 7344128 | tf_op jit(solution)/shard_map/dot_general | solution.py:11
  12.7 2.1 %fusion.24 = f32[384,512]{1,0:T(8,128)} fusion(s32[]{:T(128)S(6)} %select_n.224, f32[512,512]{1,0:T(8,128)S(1)} %fusion.11, f32[256,512]{1,0:T(8,128)} %fusion.17), kind=kLoop, calls=%fused_computation.25 | loop fusion | flops 196608 | bytes 2359300 | tf_op jit(solution)/shard_map/concatenate | solution.py:109
  14.8 2.6 %collective-permute-done = f32[384,512]{1,0:T(8,128)} collective-permute-done((f32[384,512]{1,0:T(8,128)}, f32[384,512]{1,0:T(8,128)}, u32[]{:S(2)}, u32[]{:S(2)}) %collective-permute-start) | collective-permute-done | bytes 786464 | tf_op jit(solution)/shard_map/ppermute | solution.py:50
  19.8 3.0 %collective-permute-start.1 = (f32[96,512]{1,0:T(8,128)S(1)}, f32[96,512]{1,0:T(8,128)S(1)}, u32[]{:S(2)}, u32[]{:S(2)}) collective-permute-start(f32[96,512]{1,0:T(8,128)S(1)} %get-tuple-element.21), channel_id=1, source_target_pairs={{0,2},{1,3},{2,0},{3,1},{4,6},{5,7},{6,4},{7,5},{8,10},{9,11},{10,... | collective-permute-start | bytes 589832 | tf_op jit(solution)/shard_map/ppermute | solution.py:50
  24.3 4.1 %collective-permute-done.1 = f32[96,512]{1,0:T(8,128)S(1)} collective-permute-done((f32[96,512]{1,0:T(8,128)S(1)}, f32[96,512]{1,0:T(8,128)S(1)}, u32[]{:S(2)}, u32[]{:S(2)}) %collective-permute-start.1) | collective-permute-done | bytes 196640 | tf_op jit(solution)/shard_map/ppermute | solution.py:50
  28.4 5.3 %collective-permute-done.2 = f32[96,512]{1,0:T(8,128)S(1)} collective-permute-done((f32[96,512]{1,0:T(8,128)S(1)}, f32[96,512]{1,0:T(8,128)S(1)}, u32[]{:S(2)}, u32[]{:S(2)}) %collective-permute-start.2) | collective-permute-done | bytes 196640 | tf_op jit(solution)/shard_map/ppermute | solution.py:50
  36.4 2.6 %collective-permute-start.5 = (f32[24,512]{1,0:T(8,128)S(1)}, f32[24,512]{1,0:T(8,128)S(1)}, u32[]{:S(2)}, u32[]{:S(2)}) collective-permute-start(f32[24,512]{1,0:T(8,128)S(1)} %get-tuple-element.30), channel_id=1, source_target_pairs={{0,16},{1,17},{2,18},{3,19},{4,20},{5,21},{6,22},{7,23},{8,24},{9,... | collective-permute-start | bytes 147464 | tf_op jit(solution)/shard_map/ppermute | solution.py:50
  39.2 2.7 %collective-permute-done.5 = f32[24,512]{1,0:T(8,128)S(1)} collective-permute-done((f32[24,512]{1,0:T(8,128)S(1)}, f32[24,512]{1,0:T(8,128)S(1)}, u32[]{:S(2)}, u32[]{:S(2)}) %collective-permute-start.5) | collective-permute-done | bytes 49184 | tf_op jit(solution)/shard_map/ppermute | solution.py:50
  41.9 3.5 %collective-permute-done.6 = f32[24,512]{1,0:T(8,128)S(1)} collective-permute-done((f32[24,512]{1,0:T(8,128)S(1)}, f32[24,512]{1,0:T(8,128)S(1)}, u32[]{:S(2)}, u32[]{:S(2)}) %collective-permute-start.6) | collective-permute-done | bytes 49184 | tf_op jit(solution)/shard_map/ppermute | solution.py:50
  46.2 3.7 %collective-permute-start.9 = (f32[24,512]{1,0:T(8,128)S(1)}, f32[24,512]{1,0:T(8,128)S(1)}, u32[]{:S(2)}, u32[]{:S(2)}) collective-permute-start(f32[24,512]{1,0:T(8,128)S(1)} %add_add_fusion.1), channel_id=1, source_target_pairs={{0,24},{1,25},{2,26},{3,27},{4,28},{5,29},{6,30},{7,31},{8,16},{9,... | collective-permute-start | bytes 147464 | tf_op jit(solution)/shard_map/ppermute | solution.py:58
  50.6 1.9 %collective-permute-done.9 = f32[24,512]{1,0:T(8,128)S(1)} collective-permute-done((f32[24,512]{1,0:T(8,128)S(1)}, f32[24,512]{1,0:T(8,128)S(1)}, u32[]{:S(2)}, u32[]{:S(2)}) %collective-permute-start.9) | collective-permute-done | bytes 49184 | tf_op jit(solution)/shard_map/ppermute | solution.py:58
  56.1 2.2 %collective-permute-done.10 = f32[96,512]{1,0:T(8,128)S(1)} collective-permute-done((f32[96,512]{1,0:T(8,128)S(1)}, f32[96,512]{1,0:T(8,128)S(1)}, u32[]{:S(2)}, u32[]{:S(2)}) %collective-permute-start.10) | collective-permute-done | bytes 196640 | tf_op jit(solution)/shard_map/ppermute | solution.py:58
  58.3 3.3 %collective-permute-done.11 = f32[96,512]{1,0:T(8,128)S(1)} collective-permute-done((f32[96,512]{1,0:T(8,128)S(1)}, f32[96,512]{1,0:T(8,128)S(1)}, u32[]{:S(2)}, u32[]{:S(2)}) %collective-permute-start.11) | collective-permute-done | bytes 196640 | tf_op jit(solution)/shard_map/ppermute | solution.py:58
  64.3 2.6 %collective-permute-done.13 = f32[384,512]{1,0:T(8,128)} collective-permute-done((f32[384,512]{1,0:T(8,128)}, f32[384,512]{1,0:T(8,128)}, u32[]{:S(2)}, u32[]{:S(2)}) %collective-permute-start.13) | collective-permute-done | bytes 786464 | tf_op jit(solution)/shard_map/ppermute | solution.py:58
  66.9 2.3 %broadcast_select_fusion.1 = (f32[384,512]{1,0:T(8,128)S(1)}, f32[384,512]{1,0:T(8,128)}) fusion(f32[384,512]{1,0:T(8,128)} %collective-permute-done.13, pred[]{:T(512)S(6)} %eq.84, f32[96,512]{1,0:T(8,128)} %copy-done.5, f32[96,512]{1,0:T(8,128)S(1)} %get-tuple-element.20, f32[96,512]{1,0:T(8,128)S(1)} %get-tuple-element.19, f32[96,512]{1,0:T(8,128)} %copy-done.4, ...), kind=kLoop, calls=%fused_computation.32 | loop fusion | flops 983040 | bytes 3145730 | tf_op jit(solution)/shard_map/jit(_where)/select_n | solution.py:34
  69.2 11.7 %custom-call.22 = f32[128,128]{1,0:T(8,128)S(1)} custom-call(f32[128,128]{1,0:T(8,128)S(1)} %slice.100), custom_call_target="Cholesky" | custom-call | tf_op jit(solution)/shard_map/cholesky/custom-call.1 | solution.py:117
  82.9 9.9 %custom-call.15 = f32[1,128,128]{1,2,0:T(8,128)S(1)} custom-call(f32[1,128,128]{2,1,0:T(8,128)S(1)} %get-tuple-element.11), custom_call_target="InvertDiagBlocksLowerTriangular" | custom-call | tf_op jit(solution)/shard_map/triangular_solve | solution.py:118
  96.2 11.7 %custom-call.23 = f32[128,128]{1,0:T(8,128)S(1)} custom-call(f32[128,128]{1,0:T(8,128)S(1)} %slice.102), custom_call_target="Cholesky" | custom-call | tf_op jit(solution)/shard_map/cholesky/custom-call.1 | solution.py:117
  109.8 9.8 %custom-call.16 = f32[1,128,128]{1,2,0:T(8,128)S(1)} custom-call(f32[1,128,128]{2,1,0:T(8,128)S(1)} %get-tuple-element.9), custom_call_target="InvertDiagBlocksLowerTriangular" | custom-call | tf_op jit(solution)/shard_map/triangular_solve | solution.py:118
  122.6 11.9 %custom-call.24 = f32[128,128]{1,0:T(8,128)S(1)} custom-call(f32[128,128]{1,0:T(8,128)S(1)} %slice.105), custom_call_target="Cholesky" | custom-call | tf_op jit(solution)/shard_map/cholesky/custom-call.1 | solution.py:117
  136.4 9.8 %custom-call.17 = f32[1,128,128]{1,2,0:T(8,128)S(1)} custom-call(f32[1,128,128]{2,1,0:T(8,128)S(1)} %get-tuple-element.7), custom_call_target="InvertDiagBlocksLowerTriangular" | custom-call | tf_op jit(solution)/shard_map/triangular_solve | solution.py:118
  148.3 11.7 %custom-call.25 = f32[128,128]{1,0:T(8,128)S(1)} custom-call(f32[128,128]{1,0:T(8,128)S(1)} %slice.108), custom_call_target="Cholesky" | custom-call | tf_op jit(solution)/shard_map/cholesky/custom-call.1 | solution.py:117
  162.1 9.8 %custom-call.18 = f32[1,128,128]{1,2,0:T(8,128)S(1)} custom-call(f32[1,128,128]{2,1,0:T(8,128)S(1)} %get-tuple-element.5), custom_call_target="InvertDiagBlocksLowerTriangular" | custom-call | tf_op jit(solution)/shard_map/triangular_solve | solution.py:118
  (94 shorter events, 39.2 us)
Async XLA Ops:
  0.6 9.4 %copy-start = (bf16[4096,256]{1,0:T(8,128)(2,1)S(1)}, bf16[4096,256]{1,0:T(8,128)(2,1)}, u32[]{:S(2)}) copy-start(bf16[4096,256]{1,0:T(8,128)(2,1)} %param.8) | copy-start | bytes 6291460
  0.6 2.9 %copy-start.9 = (s32[4096]{0:T(1024)S(1)}, s32[4096]{0:T(1024)}, u32[]{:S(2)}) copy-start(s32[4096]{0:T(1024)} %param.9) | copy-start | bytes 49156
  3.6 6.4 %copy-start.10 = (bf16[4096,512]{1,0:T(8,128)(2,1)S(1)}, bf16[4096,512]{1,0:T(8,128)(2,1)}, u32[]{:S(2)}) copy-start(bf16[4096,512]{1,0:T(8,128)(2,1)} %param.7) | copy-start | bytes 12582916
  14.8 2.6 %collective-permute-start = (f32[384,512]{1,0:T(8,128)}, f32[384,512]{1,0:T(8,128)}, u32[]{:S(2)}, u32[]{:S(2)}) collective-permute-start(f32[384,512]{1,0:T(8,128)} %fusion.24), channel_id=1, source_target_pairs={{0,1},{1,0},{2,3},{3,2},{4,5},{5,4},{6,7},{7,6},{8,9},{9,8},{10,11... | collective-permute-start | bytes 2359304 | tf_op jit(solution)/shard_map/ppermute | solution.py:50
  18.8 0.9 copy-start.3
  19.8 8.7 %collective-permute-start.1 = (f32[96,512]{1,0:T(8,128)S(1)}, f32[96,512]{1,0:T(8,128)S(1)}, u32[]{:S(2)}, u32[]{:S(2)}) collective-permute-start(f32[96,512]{1,0:T(8,128)S(1)} %get-tuple-element.21), channel_id=1, source_target_pairs={{0,2},{1,3},{2,0},{3,1},{4,6},{5,7},{6,4},{7,5},{8,10},{9,11},{10,... | collective-permute-start | bytes 589832 | tf_op jit(solution)/shard_map/ppermute | solution.py:50
  22.8 11.0 %collective-permute-start.2 = (f32[96,512]{1,0:T(8,128)S(1)}, f32[96,512]{1,0:T(8,128)S(1)}, u32[]{:S(2)}, u32[]{:S(2)}) collective-permute-start(f32[96,512]{1,0:T(8,128)S(1)} %get-tuple-element.23), channel_id=1, source_target_pairs={{0,4},{1,5},{2,6},{3,7},{4,0},{5,1},{6,2},{7,3},{8,12},{9,13},{10,... | collective-permute-start | bytes 589832 | tf_op jit(solution)/shard_map/ppermute | solution.py:50
  24.3 9.5 %collective-permute-start.3 = (f32[96,512]{1,0:T(8,128)S(1)}, f32[96,512]{1,0:T(8,128)S(1)}, u32[]{:S(2)}, u32[]{:S(2)}) collective-permute-start(f32[96,512]{1,0:T(8,128)S(1)} %get-tuple-element.22), channel_id=1, source_target_pairs={{0,6},{1,7},{2,4},{3,5},{4,2},{5,3},{6,0},{7,1},{8,14},{9,15},{10,... | collective-permute-start | bytes 589832 | tf_op jit(solution)/shard_map/ppermute | solution.py:50
  34.8 4.5 %collective-permute-start.4 = (f32[24,512]{1,0:T(8,128)S(1)}, f32[24,512]{1,0:T(8,128)S(1)}, u32[]{:S(2)}, u32[]{:S(2)}) collective-permute-start(f32[24,512]{1,0:T(8,128)S(1)} %get-tuple-element.28), channel_id=1, source_target_pairs={{0,8},{1,9},{2,10},{3,11},{4,12},{5,13},{6,14},{7,15},{8,0},{9,1},... | collective-permute-start | bytes 147464 | tf_op jit(solution)/shard_map/ppermute | solution.py:50
  36.4 5.5 %collective-permute-start.5 = (f32[24,512]{1,0:T(8,128)S(1)}, f32[24,512]{1,0:T(8,128)S(1)}, u32[]{:S(2)}, u32[]{:S(2)}) collective-permute-start(f32[24,512]{1,0:T(8,128)S(1)} %get-tuple-element.30), channel_id=1, source_target_pairs={{0,16},{1,17},{2,18},{3,19},{4,20},{5,21},{6,22},{7,23},{8,24},{9,... | collective-permute-start | bytes 147464 | tf_op jit(solution)/shard_map/ppermute | solution.py:50
  39.0 6.4 %collective-permute-start.6 = (f32[24,512]{1,0:T(8,128)S(1)}, f32[24,512]{1,0:T(8,128)S(1)}, u32[]{:S(2)}, u32[]{:S(2)}) collective-permute-start(f32[24,512]{1,0:T(8,128)S(1)} %get-tuple-element.29), channel_id=1, source_target_pairs={{0,24},{1,25},{2,26},{3,27},{4,28},{5,29},{6,30},{7,31},{8,16},{9,... | collective-permute-start | bytes 147464 | tf_op jit(solution)/shard_map/ppermute | solution.py:50
  45.4 4.5 %collective-permute-start.7 = (f32[24,512]{1,0:T(8,128)S(1)}, f32[24,512]{1,0:T(8,128)S(1)}, u32[]{:S(2)}, u32[]{:S(2)}) collective-permute-start(f32[24,512]{1,0:T(8,128)S(1)} %add_add_fusion.1), channel_id=1, source_target_pairs={{0,8},{1,9},{2,10},{3,11},{4,12},{5,13},{6,14},{7,15},{8,0},{9,1},... | collective-permute-start | bytes 147464 | tf_op jit(solution)/shard_map/ppermute | solution.py:58
  45.5 5.1 %collective-permute-start.8 = (f32[24,512]{1,0:T(8,128)S(1)}, f32[24,512]{1,0:T(8,128)S(1)}, u32[]{:S(2)}, u32[]{:S(2)}) collective-permute-start(f32[24,512]{1,0:T(8,128)S(1)} %add_add_fusion.1), channel_id=1, source_target_pairs={{0,16},{1,17},{2,18},{3,19},{4,20},{5,21},{6,22},{7,23},{8,24},{9,... | collective-permute-start | bytes 147464 | tf_op jit(solution)/shard_map/ppermute | solution.py:58
  46.2 6.3 %collective-permute-start.9 = (f32[24,512]{1,0:T(8,128)S(1)}, f32[24,512]{1,0:T(8,128)S(1)}, u32[]{:S(2)}, u32[]{:S(2)}) collective-permute-start(f32[24,512]{1,0:T(8,128)S(1)} %add_add_fusion.1), channel_id=1, source_target_pairs={{0,24},{1,25},{2,26},{3,27},{4,28},{5,29},{6,30},{7,31},{8,16},{9,... | collective-permute-start | bytes 147464 | tf_op jit(solution)/shard_map/ppermute | solution.py:58
  52.5 5.7 %collective-permute-start.10 = (f32[96,512]{1,0:T(8,128)S(1)}, f32[96,512]{1,0:T(8,128)S(1)}, u32[]{:S(2)}, u32[]{:S(2)}) collective-permute-start(f32[96,512]{1,0:T(8,128)S(1)} %pad_maximum_fusion.3), channel_id=1, source_target_pairs={{0,2},{1,3},{2,0},{3,1},{4,6},{5,7},{6,4},{7,5},{8,10},{9,11},{10,... | collective-permute-start | bytes 589832 | tf_op jit(solution)/shard_map/ppermute | solution.py:58
  53.8 7.8 %collective-permute-start.11 = (f32[96,512]{1,0:T(8,128)S(1)}, f32[96,512]{1,0:T(8,128)S(1)}, u32[]{:S(2)}, u32[]{:S(2)}) collective-permute-start(f32[96,512]{1,0:T(8,128)S(1)} %pad_maximum_fusion.3), channel_id=1, source_target_pairs={{0,4},{1,5},{2,6},{3,7},{4,0},{5,1},{6,2},{7,3},{8,12},{9,13},{10,... | collective-permute-start | bytes 589832 | tf_op jit(solution)/shard_map/ppermute | solution.py:58
  54.5 7.0 %collective-permute-start.12 = (f32[96,512]{1,0:T(8,128)S(1)}, f32[96,512]{1,0:T(8,128)S(1)}, u32[]{:S(2)}, u32[]{:S(2)}) collective-permute-start(f32[96,512]{1,0:T(8,128)S(1)} %pad_maximum_fusion.3), channel_id=1, source_target_pairs={{0,6},{1,7},{2,4},{3,5},{4,2},{5,3},{6,0},{7,1},{8,14},{9,15},{10,... | collective-permute-start | bytes 589832 | tf_op jit(solution)/shard_map/ppermute | solution.py:58
  63.3 1.0 copy-start.4
  63.3 1.0 copy-start.5
  64.3 2.6 %collective-permute-start.13 = (f32[384,512]{1,0:T(8,128)}, f32[384,512]{1,0:T(8,128)}, u32[]{:S(2)}, u32[]{:S(2)}) collective-permute-start(f32[384,512]{1,0:T(8,128)} %pad_maximum_fusion.2), channel_id=1, source_target_pairs={{0,1},{1,0},{2,3},{3,2},{4,5},{5,4},{6,7},{7,6},{8,9},{9,8},{10,11... | collective-permute-start | bytes 2359304 | tf_op jit(solution)/shard_map/ppermute | solution.py:58
  92.8 1.4 copy-start.1
  95.2 0.9 copy-start.2
  146.9 1.4 copy-start.6
  174.1 1.9 %copy-start.8 = (f32[128,128]{1,0:T(8,128)S(1)}, f32[128,128]{1,0:T(8,128)}, u32[]{:S(2)}) copy-start(f32[128,128]{1,0:T(8,128)} %get-tuple-element.6) | copy-start | bytes 196612
  (1 other events, 0.7 us)

commit v3 on v1

--- a/solution.py
+++ b/solution.py
@@ -118,7 +118,7 @@
         panel = lax.linalg.triangular_solve(
             diag, trail[block:, :block], left_side=False, lower=True, transpose_a=True
         )
-        columns.append(jnp.concatenate([jnp.tril(diag), panel], axis=0))
+        columns.append(jnp.concatenate([diag, panel], axis=0))
         if s + block < n:
             upper = panel[: n - s - block]
             trail = trail[block:, block:] - lax.dot_general(
@@ -128,9 +128,11 @@
                 precision=lax.Precision.HIGHEST,
                 preferred_element_type=jnp.float32,
             )
-    lower = jnp.concatenate(
-        [jnp.pad(col[: n - s], ((s, 0), (0, 0))) for s, col in zip(range(0, n, block), columns)],
-        axis=1,
+    lower = jnp.tril(
+        jnp.concatenate(
+            [jnp.pad(col[: n - s], ((s, 0), (0, 0))) for s, col in zip(range(0, n, block), columns)],
+            axis=1,
+        )
     )
     new_z_t = jnp.concatenate([col[n - s :] for s, col in zip(range(0, n, block), columns)], axis=1)
     return (lower.T, new_z_t.T)

time: 181 us -> 176 us (0.972)
  other arithmetic: 108 us -> 105 us
    select_n x4 -> x0, other arithmetic: 5.14 us -> none  [factor_and_solve(): columns.append(jnp.concatenate([jnp.tril(diag), panel], axis=0))]
    another operation x8, other arithmetic: 42.4 us -> 44.5 us  [factor_and_solve(): lax.linalg.triangular_solve(diag, trail[block:, :block], left_side=False,...]
where the time goes in v3:
time: 176 us; the launch traced here: 175 us
  other arithmetic  105 us (60%)
  waiting for transfers between devices  27.8 us (16%)
  starting transfers between devices  17.7 us (10%)
  matrix products  17.5 us (10%)
  local copies, waits for them, and re-layouts  5.37 us (3%)
    another operation x12, other arithmetic, factor_and_solve(): diag = lax.linalg.cholesky_p.bind(trail[:block, :block])  49.8 us
    another operation x8, other arithmetic, factor_and_solve(): lax.linalg.triangular_solve(diag, trail[block:, :block], left_side=False,...  44.5 us
    ppermute x7, waiting for transfers between devices, exchange_sum(): acc = acc + lax.ppermute(pick(parts, digit ^ a), AXES, pairs)  17.2 us
    ppermute x7, waiting for transfers between devices, exchange_sum(): got.append(lax.ppermute(cur, AXES, pairs))  10.6 us
    ppermute x7, starting transfers between devices, exchange_sum(): acc = acc + lax.ppermute(pick(parts, digit ^ a), AXES, pairs)  9.64 us
    dot_general x2, matrix products, contract(): lax.dot_general(left, right, (((0,), (0,)), ((), ())), precision=precisio...  9.04 us
    ppermute x7, starting transfers between devices, exchange_sum(): got.append(lax.ppermute(cur, AXES, pairs))  8.07 us
    another operation x4, matrix products, factor_and_solve(): lax.linalg.triangular_solve(diag, trail[block:, :block], left_side=False,...  4.13 us
  transfers between devices with their start and end apart: 14, of which 11 were waited for; matrix products, arithmetic and copies ran while one was open for 0% of the time, Pallas kernels for 0%

profile of v3, /device:TPU:0, one launch (start us, length us, event | category | flops | bytes accessed | tf_op | source)
XLA Modules:
  0.0 175.4 jit_solution(14900009863100675625)
XLA Ops:
  4.3 6.4 %fusion.11 = f32[512,512]{1,0:T(8,128)S(1)} fusion(bf16[4096,512]{1,0:T(8,128)(2,1)} %param.7, pred[4096]{0:T(1024)(128)(4,1)S(1)} %fusion.62, f32[512,768]{0,1:T(8,128)S(1)} %fusion.66), kind=kOutput, calls=%fused_computation.9 | convolution fusion | flops 2149842944 | bytes 10489856 | tf_op jit(solution)/shard_map/dot_general | solution.py:11
  10.8 2.6 %fusion.17 = f32[256,512]{1,0:T(8,128)} fusion(bf16[4096,256]{1,0:T(8,128)(2,1)S(1)} %copy-done, bf16[4096,512]{1,0:T(8,128)(2,1)S(1)} %copy-done.4, pred[4096]{0:T(1024)(128)(4,1)S(1)} %fusion.62, f32[512,768]{0,1:T(8,128)S(1)} %fusion.66), kind=kOutput, calls=%fused_computation.11 | convolution fusion | flops 1075970048 | bytes 7344128 | tf_op jit(solution)/shard_map/dot_general | solution.py:11
  13.4 2.1 %slice_select_fusion = f32[384,512]{1,0:T(8,128)} fusion(f32[512,512]{1,0:T(8,128)S(1)} %fusion.11, pred[]{:T(512)S(6)} %eq.115, f32[256,512]{1,0:T(8,128)} %fusion.17), kind=kLoop, calls=%fused_computation.26 | loop fusion | flops 393216 | bytes 3145729 | tf_op jit(solution)/shard_map/jit(_where)/select_n | solution.py:34
  15.9 2.3 %collective-permute-done = f32[384,512]{1,0:T(8,128)} collective-permute-done((f32[384,512]{1,0:T(8,128)}, f32[384,512]{1,0:T(8,128)}, u32[]{:S(2)}, u32[]{:S(2)}) %collective-permute-start) | collective-permute-done | bytes 786464 | tf_op jit(solution)/shard_map/ppermute | solution.py:50
  19.7 2.9 %collective-permute-start.1 = (f32[96,512]{1,0:T(8,128)S(1)}, f32[96,512]{1,0:T(8,128)S(1)}, u32[]{:S(2)}, u32[]{:S(2)}) collective-permute-start(f32[96,512]{1,0:T(8,128)S(1)} %get-tuple-element.21), channel_id=1, source_target_pairs={{0,2},{1,3},{2,0},{3,1},{4,6},{5,7},{6,4},{7,5},{8,10},{9,11},{10,... | collective-permute-start | bytes 589832 | tf_op jit(solution)/shard_map/ppermute | solution.py:50
  24.5 3.9 %collective-permute-done.1 = f32[96,512]{1,0:T(8,128)S(1)} collective-permute-done((f32[96,512]{1,0:T(8,128)S(1)}, f32[96,512]{1,0:T(8,128)S(1)}, u32[]{:S(2)}, u32[]{:S(2)}) %collective-permute-start.1) | collective-permute-done | bytes 196640 | tf_op jit(solution)/shard_map/ppermute | solution.py:50
  28.4 5.2 %collective-permute-done.2 = f32[96,512]{1,0:T(8,128)S(1)} collective-permute-done((f32[96,512]{1,0:T(8,128)S(1)}, f32[96,512]{1,0:T(8,128)S(1)}, u32[]{:S(2)}, u32[]{:S(2)}) %collective-permute-start.2) | collective-permute-done | bytes 196640 | tf_op jit(solution)/shard_map/ppermute | solution.py:50
  36.6 2.6 %collective-permute-start.5 = (f32[24,512]{1,0:T(8,128)S(1)}, f32[24,512]{1,0:T(8,128)S(1)}, u32[]{:S(2)}, u32[]{:S(2)}) collective-permute-start(f32[24,512]{1,0:T(8,128)S(1)} %get-tuple-element.28), channel_id=1, source_target_pairs={{0,16},{1,17},{2,18},{3,19},{4,20},{5,21},{6,22},{7,23},{8,24},{9,... | collective-permute-start | bytes 147464 | tf_op jit(solution)/shard_map/ppermute | solution.py:50
  39.5 2.6 %collective-permute-done.5 = f32[24,512]{1,0:T(8,128)S(1)} collective-permute-done((f32[24,512]{1,0:T(8,128)S(1)}, f32[24,512]{1,0:T(8,128)S(1)}, u32[]{:S(2)}, u32[]{:S(2)}) %collective-permute-start.5) | collective-permute-done | bytes 49184 | tf_op jit(solution)/shard_map/ppermute | solution.py:50
  42.1 3.3 %collective-permute-done.6 = f32[24,512]{1,0:T(8,128)S(1)} collective-permute-done((f32[24,512]{1,0:T(8,128)S(1)}, f32[24,512]{1,0:T(8,128)S(1)}, u32[]{:S(2)}, u32[]{:S(2)}) %collective-permute-start.6) | collective-permute-done | bytes 49184 | tf_op jit(solution)/shard_map/ppermute | solution.py:50
  46.3 3.5 %collective-permute-start.9 = (f32[24,512]{1,0:T(8,128)S(1)}, f32[24,512]{1,0:T(8,128)S(1)}, u32[]{:S(2)}, u32[]{:S(2)}) collective-permute-start(f32[24,512]{1,0:T(8,128)S(1)} %add_add_fusion.1), channel_id=1, source_target_pairs={{0,24},{1,25},{2,26},{3,27},{4,28},{5,29},{6,30},{7,31},{8,16},{9,... | collective-permute-start | bytes 147464 | tf_op jit(solution)/shard_map/ppermute | solution.py:58
  50.5 1.9 %collective-permute-done.9 = f32[24,512]{1,0:T(8,128)S(1)} collective-permute-done((f32[24,512]{1,0:T(8,128)S(1)}, f32[24,512]{1,0:T(8,128)S(1)}, u32[]{:S(2)}, u32[]{:S(2)}) %collective-permute-start.9) | collective-permute-done | bytes 49184 | tf_op jit(solution)/shard_map/ppermute | solution.py:58
  56.0 2.2 %collective-permute-done.10 = f32[96,512]{1,0:T(8,128)S(1)} collective-permute-done((f32[96,512]{1,0:T(8,128)S(1)}, f32[96,512]{1,0:T(8,128)S(1)}, u32[]{:S(2)}, u32[]{:S(2)}) %collective-permute-start.10) | collective-permute-done | bytes 196640 | tf_op jit(solution)/shard_map/ppermute | solution.py:58
  58.2 3.5 %collective-permute-done.11 = f32[96,512]{1,0:T(8,128)S(1)} collective-permute-done((f32[96,512]{1,0:T(8,128)S(1)}, f32[96,512]{1,0:T(8,128)S(1)}, u32[]{:S(2)}, u32[]{:S(2)}) %collective-permute-start.11) | collective-permute-done | bytes 196640 | tf_op jit(solution)/shard_map/ppermute | solution.py:58
  62.0 2.3 %collective-permute-done.13 = f32[384,512]{1,0:T(8,128)S(1)} collective-permute-done((f32[384,512]{1,0:T(8,128)S(1)}, f32[384,512]{1,0:T(8,128)S(1)}, u32[]{:S(2)}, u32[]{:S(2)}) %collective-permute-start.13) | collective-permute-done | bytes 786464 | tf_op jit(solution)/shard_map/ppermute | solution.py:58
  65.4 11.7 %custom-call.22 = f32[128,128]{1,0:T(8,128)S(1)} custom-call(f32[128,128]{1,0:T(8,128)S(1)} %slice.149), custom_call_target="Cholesky" | custom-call | tf_op jit(solution)/shard_map/cholesky/custom-call.1 | solution.py:117
  79.0 9.9 %custom-call.15 = f32[1,128,128]{1,2,0:T(8,128)S(1)} custom-call(f32[1,128,128]{2,1,0:T(8,128)S(1)} %get-tuple-element.11), custom_call_target="InvertDiagBlocksLowerTriangular" | custom-call | tf_op jit(solution)/shard_map/triangular_solve | solution.py:118
  90.3 2.0 %fusion.24 = f32[640,384]{1,0:T(8,128)S(1)} fusion(f32[384,512]{1,0:T(8,128)} %get-tuple-element.16, f32[384,512]{1,0:T(8,128)S(1)} %get-tuple-element.15, f32[640,128]{1,0:T(8,128)S(1)} %fusion.25), kind=kOutput, calls=%fused_computation.22 | convolution fusion | flops 377978880 | bytes 3080192 | tf_op jit(solution)/shard_map/dot_general | solution.py:124
  93.3 11.7 %custom-call.23 = f32[128,128]{1,0:T(8,128)S(1)} custom-call(f32[128,128]{1,0:T(8,128)S(1)} %slice.151), custom_call_target="Cholesky" | custom-call | tf_op jit(solution)/shard_map/cholesky/custom-call.1 | solution.py:117
  107.0 9.8 %custom-call.16 = f32[1,128,128]{1,2,0:T(8,128)S(1)} custom-call(f32[1,128,128]{2,1,0:T(8,128)S(1)} %get-tuple-element.9), custom_call_target="InvertDiagBlocksLowerTriangular" | custom-call | tf_op jit(solution)/shard_map/triangular_solve | solution.py:118
  119.7 11.9 %custom-call.24 = f32[128,128]{1,0:T(8,128)S(1)} custom-call(f32[128,128]{1,0:T(8,128)S(1)} %slice.154), custom_call_target="Cholesky" | custom-call | tf_op jit(solution)/shard_map/cholesky/custom-call.1 | solution.py:117
  133.6 9.8 %custom-call.17 = f32[1,128,128]{1,2,0:T(8,128)S(1)} custom-call(f32[1,128,128]{2,1,0:T(8,128)S(1)} %get-tuple-element.7), custom_call_target="InvertDiagBlocksLowerTriangular" | custom-call | tf_op jit(solution)/shard_map/triangular_solve | solution.py:118
  145.4 11.7 %custom-call.25 = f32[128,128]{1,0:T(8,128)S(1)} custom-call(f32[128,128]{1,0:T(8,128)S(1)} %slice.157), custom_call_target="Cholesky" | custom-call | tf_op jit(solution)/shard_map/cholesky/custom-call.1 | solution.py:117
  159.2 9.8 %custom-call.18 = f32[1,128,128]{1,2,0:T(8,128)S(1)} custom-call(f32[1,128,128]{2,1,0:T(8,128)S(1)} %get-tuple-element.5), custom_call_target="InvertDiagBlocksLowerTriangular" | custom-call | tf_op jit(solution)/shard_map/triangular_solve | solution.py:118
  (84 shorter events, 38.2 us)
Async XLA Ops:
  0.6 10.1 %copy-start = (bf16[4096,256]{1,0:T(8,128)(2,1)S(1)}, bf16[4096,256]{1,0:T(8,128)(2,1)}, u32[]{:S(2)}) copy-start(bf16[4096,256]{1,0:T(8,128)(2,1)} %param.8) | copy-start | bytes 6291460
  4.3 6.4 %copy-start.4 = (bf16[4096,512]{1,0:T(8,128)(2,1)S(1)}, bf16[4096,512]{1,0:T(8,128)(2,1)}, u32[]{:S(2)}) copy-start(bf16[4096,512]{1,0:T(8,128)(2,1)} %param.7) | copy-start | bytes 12582916
  15.4 2.7 %collective-permute-start = (f32[384,512]{1,0:T(8,128)}, f32[384,512]{1,0:T(8,128)}, u32[]{:S(2)}, u32[]{:S(2)}) collective-permute-start(f32[384,512]{1,0:T(8,128)} %slice_select_fusion), channel_id=1, source_target_pairs={{0,1},{1,0},{2,3},{3,2},{4,5},{5,4},{6,7},{7,6},{8,9},{9,8},{10,11... | collective-permute-start | bytes 2359304 | tf_op jit(solution)/shard_map/ppermute | solution.py:50
  19.7 4.6 %copy-start.1 = (f32[384,512]{1,0:T(8,128)}, f32[384,512]{1,0:T(8,128)S(1)}, u32[]{:S(2)}) copy-start(f32[384,512]{1,0:T(8,128)S(1)} %select_add_fusion) | copy-start | bytes 2359300
  19.7 8.6 %collective-permute-start.1 = (f32[96,512]{1,0:T(8,128)S(1)}, f32[96,512]{1,0:T(8,128)S(1)}, u32[]{:S(2)}, u32[]{:S(2)}) collective-permute-start(f32[96,512]{1,0:T(8,128)S(1)} %get-tuple-element.21), channel_id=1, source_target_pairs={{0,2},{1,3},{2,0},{3,1},{4,6},{5,7},{6,4},{7,5},{8,10},{9,11},{10,... | collective-permute-start | bytes 589832 | tf_op jit(solution)/shard_map/ppermute | solution.py:50
  22.7 10.9 %collective-permute-start.2 = (f32[96,512]{1,0:T(8,128)S(1)}, f32[96,512]{1,0:T(8,128)S(1)}, u32[]{:S(2)}, u32[]{:S(2)}) collective-permute-start(f32[96,512]{1,0:T(8,128)S(1)} %get-tuple-element.22), channel_id=1, source_target_pairs={{0,4},{1,5},{2,6},{3,7},{4,0},{5,1},{6,2},{7,3},{8,12},{9,13},{10,... | collective-permute-start | bytes 589832 | tf_op jit(solution)/shard_map/ppermute | solution.py:50
  24.3 9.3 %collective-permute-start.3 = (f32[96,512]{1,0:T(8,128)S(1)}, f32[96,512]{1,0:T(8,128)S(1)}, u32[]{:S(2)}, u32[]{:S(2)}) collective-permute-start(f32[96,512]{1,0:T(8,128)S(1)} %select_select_fusion.4), channel_id=1, source_target_pairs={{0,6},{1,7},{2,4},{3,5},{4,2},{5,3},{6,0},{7,1},{8,14},{9,15},{10,... | collective-permute-start | bytes 589832 | tf_op jit(solution)/shard_map/ppermute | solution.py:50
  34.9 4.6 %collective-permute-start.4 = (f32[24,512]{1,0:T(8,128)S(1)}, f32[24,512]{1,0:T(8,128)S(1)}, u32[]{:S(2)}, u32[]{:S(2)}) collective-permute-start(f32[24,512]{1,0:T(8,128)S(1)} %get-tuple-element.27), channel_id=1, source_target_pairs={{0,8},{1,9},{2,10},{3,11},{4,12},{5,13},{6,14},{7,15},{8,0},{9,1},... | collective-permute-start | bytes 147464 | tf_op jit(solution)/shard_map/ppermute | solution.py:50
  36.6 5.5 %collective-permute-start.5 = (f32[24,512]{1,0:T(8,128)S(1)}, f32[24,512]{1,0:T(8,128)S(1)}, u32[]{:S(2)}, u32[]{:S(2)}) collective-permute-start(f32[24,512]{1,0:T(8,128)S(1)} %get-tuple-element.28), channel_id=1, source_target_pairs={{0,16},{1,17},{2,18},{3,19},{4,20},{5,21},{6,22},{7,23},{8,24},{9,... | collective-permute-start | bytes 147464 | tf_op jit(solution)/shard_map/ppermute | solution.py:50
  39.2 6.2 %collective-permute-start.6 = (f32[24,512]{1,0:T(8,128)S(1)}, f32[24,512]{1,0:T(8,128)S(1)}, u32[]{:S(2)}, u32[]{:S(2)}) collective-permute-start(f32[24,512]{1,0:T(8,128)S(1)} %select_select_fusion.11), channel_id=1, source_target_pairs={{0,24},{1,25},{2,26},{3,27},{4,28},{5,29},{6,30},{7,31},{8,16},{9,... | collective-permute-start | bytes 147464 | tf_op jit(solution)/shard_map/ppermute | solution.py:50
  45.4 4.5 %collective-permute-start.7 = (f32[24,512]{1,0:T(8,128)S(1)}, f32[24,512]{1,0:T(8,128)S(1)}, u32[]{:S(2)}, u32[]{:S(2)}) collective-permute-start(f32[24,512]{1,0:T(8,128)S(1)} %add_add_fusion.1), channel_id=1, source_target_pairs={{0,8},{1,9},{2,10},{3,11},{4,12},{5,13},{6,14},{7,15},{8,0},{9,1},... | collective-permute-start | bytes 147464 | tf_op jit(solution)/shard_map/ppermute | solution.py:58
  45.5 5.1 %collective-permute-start.8 = (f32[24,512]{1,0:T(8,128)S(1)}, f32[24,512]{1,0:T(8,128)S(1)}, u32[]{:S(2)}, u32[]{:S(2)}) collective-permute-start(f32[24,512]{1,0:T(8,128)S(1)} %add_add_fusion.1), channel_id=1, source_target_pairs={{0,16},{1,17},{2,18},{3,19},{4,20},{5,21},{6,22},{7,23},{8,24},{9,... | collective-permute-start | bytes 147464 | tf_op jit(solution)/shard_map/ppermute | solution.py:58
  46.3 6.1 %collective-permute-start.9 = (f32[24,512]{1,0:T(8,128)S(1)}, f32[24,512]{1,0:T(8,128)S(1)}, u32[]{:S(2)}, u32[]{:S(2)}) collective-permute-start(f32[24,512]{1,0:T(8,128)S(1)} %add_add_fusion.1), channel_id=1, source_target_pairs={{0,24},{1,25},{2,26},{3,27},{4,28},{5,29},{6,30},{7,31},{8,16},{9,... | collective-permute-start | bytes 147464 | tf_op jit(solution)/shard_map/ppermute | solution.py:58
  52.5 5.7 %collective-permute-start.10 = (f32[96,512]{1,0:T(8,128)S(1)}, f32[96,512]{1,0:T(8,128)S(1)}, u32[]{:S(2)}, u32[]{:S(2)}) collective-permute-start(f32[96,512]{1,0:T(8,128)S(1)} %pad_maximum_fusion.4), channel_id=1, source_target_pairs={{0,2},{1,3},{2,0},{3,1},{4,6},{5,7},{6,4},{7,5},{8,10},{9,11},{10,... | collective-permute-start | bytes 589832 | tf_op jit(solution)/shard_map/ppermute | solution.py:58
  54.0 7.8 %collective-permute-start.11 = (f32[96,512]{1,0:T(8,128)S(1)}, f32[96,512]{1,0:T(8,128)S(1)}, u32[]{:S(2)}, u32[]{:S(2)}) collective-permute-start(f32[96,512]{1,0:T(8,128)S(1)} %pad_maximum_fusion.4), channel_id=1, source_target_pairs={{0,4},{1,5},{2,6},{3,7},{4,0},{5,1},{6,2},{7,3},{8,12},{9,13},{10,... | collective-permute-start | bytes 589832 | tf_op jit(solution)/shard_map/ppermute | solution.py:58
  54.6 7.1 %collective-permute-start.12 = (f32[96,512]{1,0:T(8,128)S(1)}, f32[96,512]{1,0:T(8,128)S(1)}, u32[]{:S(2)}, u32[]{:S(2)}) collective-permute-start(f32[96,512]{1,0:T(8,128)S(1)} %pad_maximum_fusion.4), channel_id=1, source_target_pairs={{0,6},{1,7},{2,4},{3,5},{4,2},{5,3},{6,0},{7,1},{8,14},{9,15},{10,... | collective-permute-start | bytes 589832 | tf_op jit(solution)/shard_map/ppermute | solution.py:58
  61.9 2.4 %collective-permute-start.13 = (f32[384,512]{1,0:T(8,128)S(1)}, f32[384,512]{1,0:T(8,128)S(1)}, u32[]{:S(2)}, u32[]{:S(2)}) collective-permute-start(f32[384,512]{1,0:T(8,128)S(1)} %pad_maximum_fusion.3), channel_id=1, source_target_pairs={{0,1},{1,0},{2,3},{3,2},{4,5},{5,4},{6,7},{7,6},{8,9},{9,8},{10,11... | collective-permute-start | bytes 2359304 | tf_op jit(solution)/shard_map/ppermute | solution.py:58
  92.3 0.9 copy-start.2
  144.0 1.4 copy-start.3

commit v4 on v0

--- a/solution.py
+++ b/solution.py
@@ -128,12 +128,12 @@
                 precision=lax.Precision.HIGHEST,
                 preferred_element_type=jnp.float32,
             )
-    lower = jnp.concatenate(
-        [jnp.pad(col[: n - s], ((s, 0), (0, 0))) for s, col in zip(range(0, n, block), columns)],
-        axis=1,
+    starts = range(0, n, block)
+    new_r = jnp.concatenate(
+        [jnp.pad(col[: n - s].T, ((0, 0), (s, 0))) for s, col in zip(starts, columns)], axis=0
     )
-    new_z_t = jnp.concatenate([col[n - s :] for s, col in zip(range(0, n, block), columns)], axis=1)
-    return (lower.T, new_z_t.T)
+    new_z = jnp.concatenate([col[n - s :].T for s, col in zip(starts, columns)], axis=0)
+    return (new_r, new_z)
 
 
 def solution(mesh):

time: 176 us -> 177 us (level)
    unnamed x12 -> x14, local copies, waits for them, and re-layouts: 3.27 us -> 3.92 us
where the time goes in v4:
time: 177 us; the launch traced here: 176 us
  other arithmetic  106 us (60%)
  waiting for transfers between devices  27.8 us (16%)
  matrix products  18.4 us (10%)
  starting transfers between devices  17.7 us (10%)
  local copies, waits for them, and re-layouts  4.67 us (3%)
    another operation x12, other arithmetic, factor_and_solve(): diag = lax.linalg.cholesky(trail[:block, :block], symmetrize_input=False)  49.7 us
    another operation x8, other arithmetic, factor_and_solve(): lax.linalg.triangular_solve(diag, trail[block:, :block], left_side=False,...  45 us
    ppermute x7, waiting for transfers between devices, exchange_sum(): acc = acc + lax.ppermute(pick(parts, digit ^ a), AXES, pairs)  17.2 us
    ppermute x7, waiting for transfers between devices, exchange_sum(): got.append(lax.ppermute(cur, AXES, pairs))  10.6 us
    ppermute x7, starting transfers between devices, exchange_sum(): acc = acc + lax.ppermute(pick(parts, digit ^ a), AXES, pairs)  9.64 us
    dot_general x2, matrix products, contract(): lax.dot_general(left, right, (((0,), (0,)), ((), ())), precision=precisio...  9.04 us
    ppermute x7, starting transfers between devices, exchange_sum(): got.append(lax.ppermute(cur, AXES, pairs))  8.07 us
    another operation x4, matrix products, factor_and_solve(): lax.linalg.triangular_solve(diag, trail[block:, :block], left_side=False,...  4.96 us
  transfers between devices with their start and end apart: 14, of which 11 were waited for; matrix products, arithmetic and copies ran while one was open for 0% of the time, Pallas kernels for 0%

profile of v4, /device:TPU:0, one launch (start us, length us, event | category | flops | bytes accessed | tf_op | source)
XLA Modules:
  0.0 175.9 jit_solution(2218070388364914420)
XLA Ops:
  4.3 6.4 %fusion.11 = f32[512,512]{1,0:T(8,128)S(1)} fusion(bf16[4096,512]{1,0:T(8,128)(2,1)} %param.7, pred[4096]{0:T(1024)(128)(4,1)S(1)} %fusion.64, f32[512,768]{0,1:T(8,128)S(1)} %fusion.68), kind=kOutput, calls=%fused_computation.13 | convolution fusion | flops 2149842944 | bytes 10489856 | tf_op jit(solution)/shard_map/dot_general | solution.py:11
  10.8 2.6 %fusion.17 = f32[256,512]{1,0:T(8,128)} fusion(bf16[4096,256]{1,0:T(8,128)(2,1)S(1)} %copy-done, bf16[4096,512]{1,0:T(8,128)(2,1)S(1)} %copy-done.5, pred[4096]{0:T(1024)(128)(4,1)S(1)} %fusion.64, f32[512,768]{0,1:T(8,128)S(1)} %fusion.68), kind=kOutput, calls=%fused_computation.15 | convolution fusion | flops 1075970048 | bytes 7344128 | tf_op jit(solution)/shard_map/dot_general | solution.py:11
  13.4 2.1 %slice_select_fusion = f32[384,512]{1,0:T(8,128)} fusion(f32[512,512]{1,0:T(8,128)S(1)} %fusion.11, pred[]{:T(512)S(6)} %eq.115, f32[256,512]{1,0:T(8,128)} %fusion.17), kind=kLoop, calls=%fused_computation.28 | loop fusion | flops 393216 | bytes 3145729 | tf_op jit(solution)/shard_map/jit(_where)/select_n | solution.py:34
  15.9 2.3 %collective-permute-done = f32[384,512]{1,0:T(8,128)} collective-permute-done((f32[384,512]{1,0:T(8,128)}, f32[384,512]{1,0:T(8,128)}, u32[]{:S(2)}, u32[]{:S(2)}) %collective-permute-start) | collective-permute-done | bytes 786464 | tf_op jit(solution)/shard_map/ppermute | solution.py:50
  19.7 2.9 %collective-permute-start.1 = (f32[96,512]{1,0:T(8,128)S(1)}, f32[96,512]{1,0:T(8,128)S(1)}, u32[]{:S(2)}, u32[]{:S(2)}) collective-permute-start(f32[96,512]{1,0:T(8,128)S(1)} %get-tuple-element.19), channel_id=1, source_target_pairs={{0,2},{1,3},{2,0},{3,1},{4,6},{5,7},{6,4},{7,5},{8,10},{9,11},{10,... | collective-permute-start | bytes 589832 | tf_op jit(solution)/shard_map/ppermute | solution.py:50
  24.5 3.9 %collective-permute-done.1 = f32[96,512]{1,0:T(8,128)S(1)} collective-permute-done((f32[96,512]{1,0:T(8,128)S(1)}, f32[96,512]{1,0:T(8,128)S(1)}, u32[]{:S(2)}, u32[]{:S(2)}) %collective-permute-start.1) | collective-permute-done | bytes 196640 | tf_op jit(solution)/shard_map/ppermute | solution.py:50
  28.4 5.2 %collective-permute-done.2 = f32[96,512]{1,0:T(8,128)S(1)} collective-permute-done((f32[96,512]{1,0:T(8,128)S(1)}, f32[96,512]{1,0:T(8,128)S(1)}, u32[]{:S(2)}, u32[]{:S(2)}) %collective-permute-start.2) | collective-permute-done | bytes 196640 | tf_op jit(solution)/shard_map/ppermute | solution.py:50
  36.6 2.6 %collective-permute-start.5 = (f32[24,512]{1,0:T(8,128)S(1)}, f32[24,512]{1,0:T(8,128)S(1)}, u32[]{:S(2)}, u32[]{:S(2)}) collective-permute-start(f32[24,512]{1,0:T(8,128)S(1)} %get-tuple-element.28), channel_id=1, source_target_pairs={{0,16},{1,17},{2,18},{3,19},{4,20},{5,21},{6,22},{7,23},{8,24},{9,... | collective-permute-start | bytes 147464 | tf_op jit(solution)/shard_map/ppermute | solution.py:50
  39.5 2.6 %collective-permute-done.5 = f32[24,512]{1,0:T(8,128)S(1)} collective-permute-done((f32[24,512]{1,0:T(8,128)S(1)}, f32[24,512]{1,0:T(8,128)S(1)}, u32[]{:S(2)}, u32[]{:S(2)}) %collective-permute-start.5) | collective-permute-done | bytes 49184 | tf_op jit(solution)/shard_map/ppermute | solution.py:50
  42.1 3.3 %collective-permute-done.6 = f32[24,512]{1,0:T(8,128)S(1)} collective-permute-done((f32[24,512]{1,0:T(8,128)S(1)}, f32[24,512]{1,0:T(8,128)S(1)}, u32[]{:S(2)}, u32[]{:S(2)}) %collective-permute-start.6) | collective-permute-done | bytes 49184 | tf_op jit(solution)/shard_map/ppermute | solution.py:50
  46.3 3.5 %collective-permute-start.9 = (f32[24,512]{1,0:T(8,128)S(1)}, f32[24,512]{1,0:T(8,128)S(1)}, u32[]{:S(2)}, u32[]{:S(2)}) collective-permute-start(f32[24,512]{1,0:T(8,128)S(1)} %add_add_fusion.1), channel_id=1, source_target_pairs={{0,24},{1,25},{2,26},{3,27},{4,28},{5,29},{6,30},{7,31},{8,16},{9,... | collective-permute-start | bytes 147464 | tf_op jit(solution)/shard_map/ppermute | solution.py:58
  50.5 1.9 %collective-permute-done.9 = f32[24,512]{1,0:T(8,128)S(1)} collective-permute-done((f32[24,512]{1,0:T(8,128)S(1)}, f32[24,512]{1,0:T(8,128)S(1)}, u32[]{:S(2)}, u32[]{:S(2)}) %collective-permute-start.9) | collective-permute-done | bytes 49184 | tf_op jit(solution)/shard_map/ppermute | solution.py:58
  56.0 2.2 %collective-permute-done.10 = f32[96,512]{1,0:T(8,128)S(1)} collective-permute-done((f32[96,512]{1,0:T(8,128)S(1)}, f32[96,512]{1,0:T(8,128)S(1)}, u32[]{:S(2)}, u32[]{:S(2)}) %collective-permute-start.10) | collective-permute-done | bytes 196640 | tf_op jit(solution)/shard_map/ppermute | solution.py:58
  58.2 3.5 %collective-permute-done.11 = f32[96,512]{1,0:T(8,128)S(1)} collective-permute-done((f32[96,512]{1,0:T(8,128)S(1)}, f32[96,512]{1,0:T(8,128)S(1)}, u32[]{:S(2)}, u32[]{:S(2)}) %collective-permute-start.11) | collective-permute-done | bytes 196640 | tf_op jit(solution)/shard_map/ppermute | solution.py:58
  62.0 2.3 %collective-permute-done.13 = f32[384,512]{1,0:T(8,128)S(1)} collective-permute-done((f32[384,512]{1,0:T(8,128)S(1)}, f32[384,512]{1,0:T(8,128)S(1)}, u32[]{:S(2)}, u32[]{:S(2)}) %collective-permute-start.13) | collective-permute-done | bytes 786464 | tf_op jit(solution)/shard_map/ppermute | solution.py:58
  65.4 11.7 %custom-call.22 = f32[128,128]{1,0:T(8,128)S(1)} custom-call(f32[128,128]{1,0:T(8,128)S(1)} %slice.149), custom_call_target="Cholesky" | custom-call | tf_op jit(solution)/shard_map/cholesky/custom-call.1 | solution.py:117
  79.0 9.9 %custom-call.15 = f32[1,128,128]{1,2,0:T(8,128)S(1)} custom-call(f32[1,128,128]{2,1,0:T(8,128)S(1)} %get-tuple-element.9), custom_call_target="InvertDiagBlocksLowerTriangular" | custom-call | tf_op jit(solution)/shard_map/triangular_solve | solution.py:118
  90.3 2.0 %fusion.22 = f32[640,384]{1,0:T(8,128)S(1)} fusion(f32[384,512]{1,0:T(8,128)} %get-tuple-element.14, f32[384,512]{1,0:T(8,128)S(1)} %get-tuple-element.13, f32[640,128]{1,0:T(8,128)S(1)} %fusion.23), kind=kOutput, calls=%fused_computation.24 | convolution fusion | flops 377978880 | bytes 3080192 | tf_op jit(solution)/shard_map/dot_general | solution.py:124
  93.3 11.7 %custom-call.23 = f32[128,128]{1,0:T(8,128)S(1)} custom-call(f32[128,128]{1,0:T(8,128)S(1)} %slice.151), custom_call_target="Cholesky" | custom-call | tf_op jit(solution)/shard_map/cholesky/custom-call.1 | solution.py:117
  107.0 9.8 %custom-call.16 = f32[1,128,128]{1,2,0:T(8,128)S(1)} custom-call(f32[1,128,128]{2,1,0:T(8,128)S(1)} %get-tuple-element.7), custom_call_target="InvertDiagBlocksLowerTriangular" | custom-call | tf_op jit(solution)/shard_map/triangular_solve | solution.py:118
  119.8 11.9 %custom-call.24 = f32[128,128]{1,0:T(8,128)S(1)} custom-call(f32[128,128]{1,0:T(8,128)S(1)} %slice.154), custom_call_target="Cholesky" | custom-call | tf_op jit(solution)/shard_map/cholesky/custom-call.1 | solution.py:117
  133.6 10.4 %custom-call.17 = f32[1,128,128]{1,2,0:T(8,128)} custom-call(f32[1,128,128]{2,1,0:T(8,128)S(1)} %get-tuple-element.5), custom_call_target="InvertDiagBlocksLowerTriangular" | custom-call | tf_op jit(solution)/shard_map/triangular_solve | solution.py:118
  146.3 11.7 %custom-call.25 = f32[128,128]{1,0:T(8,128)S(1)} custom-call(f32[128,128]{1,0:T(8,128)S(1)} %slice.157), custom_call_target="Cholesky" | custom-call | tf_op jit(solution)/shard_map/cholesky/custom-call.1 | solution.py:117
  159.8 9.8 %custom-call.18 = f32[1,128,128]{1,2,0:T(8,128)S(1)} custom-call(f32[1,128,128]{2,1,0:T(8,128)S(1)} %get-tuple-element.29), custom_call_target="InvertDiagBlocksLowerTriangular" | custom-call | tf_op jit(solution)/shard_map/triangular_solve | solution.py:118
  (86 shorter events, 38.0 us)
Async XLA Ops:
  0.6 10.1 %copy-start = (bf16[4096,256]{1,0:T(8,128)(2,1)S(1)}, bf16[4096,256]{1,0:T(8,128)(2,1)}, u32[]{:S(2)}) copy-start(bf16[4096,256]{1,0:T(8,128)(2,1)} %param.8) | copy-start | bytes 6291460
  4.3 6.4 %copy-start.5 = (bf16[4096,512]{1,0:T(8,128)(2,1)S(1)}, bf16[4096,512]{1,0:T(8,128)(2,1)}, u32[]{:S(2)}) copy-start(bf16[4096,512]{1,0:T(8,128)(2,1)} %param.7) | copy-start | bytes 12582916
  15.4 2.7 %collective-permute-start = (f32[384,512]{1,0:T(8,128)}, f32[384,512]{1,0:T(8,128)}, u32[]{:S(2)}, u32[]{:S(2)}) collective-permute-start(f32[384,512]{1,0:T(8,128)} %slice_select_fusion), channel_id=1, source_target_pairs={{0,1},{1,0},{2,3},{3,2},{4,5},{5,4},{6,7},{7,6},{8,9},{9,8},{10,11... | collective-permute-start | bytes 2359304 | tf_op jit(solution)/shard_map/ppermute | solution.py:50
  19.7 4.6 %copy-start.1 = (f32[384,512]{1,0:T(8,128)}, f32[384,512]{1,0:T(8,128)S(1)}, u32[]{:S(2)}) copy-start(f32[384,512]{1,0:T(8,128)S(1)} %select_add_fusion) | copy-start | bytes 2359300
  19.7 8.6 %collective-permute-start.1 = (f32[96,512]{1,0:T(8,128)S(1)}, f32[96,512]{1,0:T(8,128)S(1)}, u32[]{:S(2)}, u32[]{:S(2)}) collective-permute-start(f32[96,512]{1,0:T(8,128)S(1)} %get-tuple-element.19), channel_id=1, source_target_pairs={{0,2},{1,3},{2,0},{3,1},{4,6},{5,7},{6,4},{7,5},{8,10},{9,11},{10,... | collective-permute-start | bytes 589832 | tf_op jit(solution)/shard_map/ppermute | solution.py:50
  22.7 10.9 %collective-permute-start.2 = (f32[96,512]{1,0:T(8,128)S(1)}, f32[96,512]{1,0:T(8,128)S(1)}, u32[]{:S(2)}, u32[]{:S(2)}) collective-permute-start(f32[96,512]{1,0:T(8,128)S(1)} %get-tuple-element.20), channel_id=1, source_target_pairs={{0,4},{1,5},{2,6},{3,7},{4,0},{5,1},{6,2},{7,3},{8,12},{9,13},{10,... | collective-permute-start | bytes 589832 | tf_op jit(solution)/shard_map/ppermute | solution.py:50
  24.3 9.3 %collective-permute-start.3 = (f32[96,512]{1,0:T(8,128)S(1)}, f32[96,512]{1,0:T(8,128)S(1)}, u32[]{:S(2)}, u32[]{:S(2)}) collective-permute-start(f32[96,512]{1,0:T(8,128)S(1)} %select_select_fusion.4), channel_id=1, source_target_pairs={{0,6},{1,7},{2,4},{3,5},{4,2},{5,3},{6,0},{7,1},{8,14},{9,15},{10,... | collective-permute-start | bytes 589832 | tf_op jit(solution)/shard_map/ppermute | solution.py:50
  34.9 4.6 %collective-permute-start.4 = (f32[24,512]{1,0:T(8,128)S(1)}, f32[24,512]{1,0:T(8,128)S(1)}, u32[]{:S(2)}, u32[]{:S(2)}) collective-permute-start(f32[24,512]{1,0:T(8,128)S(1)} %get-tuple-element.27), channel_id=1, source_target_pairs={{0,8},{1,9},{2,10},{3,11},{4,12},{5,13},{6,14},{7,15},{8,0},{9,1},... | collective-permute-start | bytes 147464 | tf_op jit(solution)/shard_map/ppermute | solution.py:50
  36.6 5.5 %collective-permute-start.5 = (f32[24,512]{1,0:T(8,128)S(1)}, f32[24,512]{1,0:T(8,128)S(1)}, u32[]{:S(2)}, u32[]{:S(2)}) collective-permute-start(f32[24,512]{1,0:T(8,128)S(1)} %get-tuple-element.28), channel_id=1, source_target_pairs={{0,16},{1,17},{2,18},{3,19},{4,20},{5,21},{6,22},{7,23},{8,24},{9,... | collective-permute-start | bytes 147464 | tf_op jit(solution)/shard_map/ppermute | solution.py:50
  39.2 6.2 %collective-permute-start.6 = (f32[24,512]{1,0:T(8,128)S(1)}, f32[24,512]{1,0:T(8,128)S(1)}, u32[]{:S(2)}, u32[]{:S(2)}) collective-permute-start(f32[24,512]{1,0:T(8,128)S(1)} %select_select_fusion.15), channel_id=1, source_target_pairs={{0,24},{1,25},{2,26},{3,27},{4,28},{5,29},{6,30},{7,31},{8,16},{9,... | collective-permute-start | bytes 147464 | tf_op jit(solution)/shard_map/ppermute | solution.py:50
  45.4 4.5 %collective-permute-start.7 = (f32[24,512]{1,0:T(8,128)S(1)}, f32[24,512]{1,0:T(8,128)S(1)}, u32[]{:S(2)}, u32[]{:S(2)}) collective-permute-start(f32[24,512]{1,0:T(8,128)S(1)} %add_add_fusion.1), channel_id=1, source_target_pairs={{0,8},{1,9},{2,10},{3,11},{4,12},{5,13},{6,14},{7,15},{8,0},{9,1},... | collective-permute-start | bytes 147464 | tf_op jit(solution)/shard_map/ppermute | solution.py:58
  45.5 5.1 %collective-permute-start.8 = (f32[24,512]{1,0:T(8,128)S(1)}, f32[24,512]{1,0:T(8,128)S(1)}, u32[]{:S(2)}, u32[]{:S(2)}) collective-permute-start(f32[24,512]{1,0:T(8,128)S(1)} %add_add_fusion.1), channel_id=1, source_target_pairs={{0,16},{1,17},{2,18},{3,19},{4,20},{5,21},{6,22},{7,23},{8,24},{9,... | collective-permute-start | bytes 147464 | tf_op jit(solution)/shard_map/ppermute | solution.py:58
  46.3 6.1 %collective-permute-start.9 = (f32[24,512]{1,0:T(8,128)S(1)}, f32[24,512]{1,0:T(8,128)S(1)}, u32[]{:S(2)}, u32[]{:S(2)}) collective-permute-start(f32[24,512]{1,0:T(8,128)S(1)} %add_add_fusion.1), channel_id=1, source_target_pairs={{0,24},{1,25},{2,26},{3,27},{4,28},{5,29},{6,30},{7,31},{8,16},{9,... | collective-permute-start | bytes 147464 | tf_op jit(solution)/shard_map/ppermute | solution.py:58
  52.5 5.7 %collective-permute-start.10 = (f32[96,512]{1,0:T(8,128)S(1)}, f32[96,512]{1,0:T(8,128)S(1)}, u32[]{:S(2)}, u32[]{:S(2)}) collective-permute-start(f32[96,512]{1,0:T(8,128)S(1)} %pad_maximum_fusion.6), channel_id=1, source_target_pairs={{0,2},{1,3},{2,0},{3,1},{4,6},{5,7},{6,4},{7,5},{8,10},{9,11},{10,... | collective-permute-start | bytes 589832 | tf_op jit(solution)/shard_map/ppermute | solution.py:58
  54.0 7.8 %collective-permute-start.11 = (f32[96,512]{1,0:T(8,128)S(1)}, f32[96,512]{1,0:T(8,128)S(1)}, u32[]{:S(2)}, u32[]{:S(2)}) collective-permute-start(f32[96,512]{1,0:T(8,128)S(1)} %pad_maximum_fusion.6), channel_id=1, source_target_pairs={{0,4},{1,5},{2,6},{3,7},{4,0},{5,1},{6,2},{7,3},{8,12},{9,13},{10,... | collective-permute-start | bytes 589832 | tf_op jit(solution)/shard_map/ppermute | solution.py:58
  54.6 7.1 %collective-permute-start.12 = (f32[96,512]{1,0:T(8,128)S(1)}, f32[96,512]{1,0:T(8,128)S(1)}, u32[]{:S(2)}, u32[]{:S(2)}) collective-permute-start(f32[96,512]{1,0:T(8,128)S(1)} %pad_maximum_fusion.6), channel_id=1, source_target_pairs={{0,6},{1,7},{2,4},{3,5},{4,2},{5,3},{6,0},{7,1},{8,14},{9,15},{10,... | collective-permute-start | bytes 589832 | tf_op jit(solution)/shard_map/ppermute | solution.py:58
  61.9 2.4 %collective-permute-start.13 = (f32[384,512]{1,0:T(8,128)S(1)}, f32[384,512]{1,0:T(8,128)S(1)}, u32[]{:S(2)}, u32[]{:S(2)}) collective-permute-start(f32[384,512]{1,0:T(8,128)S(1)} %pad_maximum_fusion.2), channel_id=1, source_target_pairs={{0,1},{1,0},{2,3},{3,2},{4,5},{5,4},{6,7},{7,6},{8,9},{9,8},{10,11... | collective-permute-start | bytes 2359304 | tf_op jit(solution)/shard_map/ppermute | solution.py:58
  92.3 0.9 copy-start.2
  145.6 0.7 copy-start.3
  146.2 27.4 %copy-start.4 = (f32[128,128]{1,0:T(8,128)S(1)}, f32[128,128]{1,0:T(8,128)}, u32[]{:S(2)}) copy-start(f32[128,128]{1,0:T(8,128)} %get-tuple-element.8) | copy-start | bytes 196612

commit v5 on v0

--- a/solution.py
+++ b/solution.py
@@ -103,10 +103,8 @@
     start = lax.axis_index("grp") * share
     r_part = lax.dynamic_slice_in_dim(old_r, start, share, 0)
     z_part = lax.dynamic_slice_in_dim(old_z, start, share, 0)
-    old = fine_product(r_part, jnp.concatenate([r_part, z_part], axis=1), 0)
-    gram = gram + old[:, :width]
-    cross = cross + old[:, width:]
-    both = summed(jnp.concatenate([gram.T, cross.T], axis=0), n_dev)
+    old_t = fine_product(jnp.concatenate([r_part, z_part], axis=1), r_part, 0)
+    both = summed(jnp.concatenate([gram.T, cross.T], axis=0) + old_t, n_dev)
     return factor_and_solve(both)
 
 

time: 176 us -> 176 us (level)
    unnamed x12 -> x16, local copies, waits for them, and re-layouts: 3.27 us -> 4.41 us
  transfers between devices with their start and end apart: 14 -> 14, of which waited for: 11 -> 10; matrix products, arithmetic and copies ran while one was open for 0% -> 0% of each run, Pallas kernels for 0% -> 0%
where the time goes in v5:
time: 176 us; the launch traced here: 175 us
  other arithmetic  104 us (59%)
  waiting for transfers between devices  28 us (16%)
  starting transfers between devices  17.6 us (10%)
  matrix products  17.5 us (10%)
  local copies, waits for them, and re-layouts  6.51 us (4%)
    another operation x12, other arithmetic, factor_and_solve(): diag = lax.linalg.cholesky(trail[:block, :block], symmetrize_input=False)  49.8 us
    another operation x8, other arithmetic, factor_and_solve(): lax.linalg.triangular_solve(diag, trail[block:, :block], left_side=False,...  44.5 us
    ppermute x7, waiting for transfers between devices, exchange_sum(): acc = acc + lax.ppermute(pick(parts, digit ^ a), AXES, pairs)  17.4 us
    ppermute x7, waiting for transfers between devices, exchange_sum(): got.append(lax.ppermute(cur, AXES, pairs))  10.6 us
    ppermute x7, starting transfers between devices, exchange_sum(): acc = acc + lax.ppermute(pick(parts, digit ^ a), AXES, pairs)  9.48 us
    dot_general x2, matrix products, contract(): lax.dot_general(left, right, (((0,), (0,)), ((), ())), precision=precisio...  9 us
    ppermute x7, starting transfers between devices, exchange_sum(): got.append(lax.ppermute(cur, AXES, pairs))  8.07 us
    unnamed x16, local copies, waits for them, and re-layouts  4.41 us
  transfers between devices with their start and end apart: 14, of which 10 were waited for; matrix products, arithmetic and copies ran while one was open for 0% of the time, Pallas kernels for 0%

profile of v5, /device:TPU:0, one launch (start us, length us, event | category | flops | bytes accessed | tf_op | source)
XLA Modules:
  0.0 175.4 jit_solution(453072171323969997)
XLA Ops:
  3.9 6.4 %fusion.8 = f32[512,512]{1,0:T(8,128)S(1)} fusion(bf16[4096,512]{1,0:T(8,128)(2,1)} %param.7, pred[4096]{0:T(1024)(128)(4,1)S(1)} %fusion.55), kind=kOutput, calls=%fused_computation.9 | convolution fusion | flops 2149580800 | bytes 5246976 | tf_op jit(solution)/shard_map/dot_general | solution.py:11
  10.3 2.6 %fusion.11 = f32[256,512]{1,0:T(8,128)} fusion(bf16[4096,256]{1,0:T(8,128)(2,1)S(1)} %copy-done, bf16[4096,512]{1,0:T(8,128)(2,1)S(1)} %copy-done.6, pred[4096]{0:T(1024)(128)(4,1)S(1)} %fusion.55), kind=kOutput, calls=%fused_computation.10 | convolution fusion | flops 1075838976 | bytes 6819840 | tf_op jit(solution)/shard_map/dot_general | solution.py:11
  16.2 2.0 %collective-permute-done = f32[384,512]{1,0:T(8,128)} collective-permute-done((f32[384,512]{1,0:T(8,128)S(1)}, f32[384,512]{1,0:T(8,128)}, u32[]{:S(2)}, u32[]{:S(2)}) %collective-permute-start) | collective-permute-done | bytes 786464 | tf_op jit(solution)/shard_map/ppermute | solution.py:50
  18.2 1.9 %select_add_fusion = f32[384,512]{1,0:T(8,128)S(1)} fusion(f32[384,512]{1,0:T(8,128)} %collective-permute-done, f32[768,512]{1,0:T(8,128)} %copy-done.1, pred[]{:T(512)S(6)} %eq.110), kind=kLoop, calls=%fused_computation.21 | loop fusion | flops 393216 | bytes 3145729 | tf_op jit(solution)/shard_map/add | solution.py:50
  20.9 2.9 %collective-permute-start.1 = (f32[96,512]{1,0:T(8,128)}, f32[96,512]{1,0:T(8,128)S(1)}, u32[]{:S(2)}, u32[]{:S(2)}) collective-permute-start(f32[96,512]{1,0:T(8,128)} %get-tuple-element.21), channel_id=1, source_target_pairs={{0,2},{1,3},{2,0},{3,1},{4,6},{5,7},{6,4},{7,5},{8,10},{9,11},{10,... | collective-permute-start | bytes 589832 | tf_op jit(solution)/shard_map/ppermute | solution.py:50
  25.4 4.2 %collective-permute-done.1 = f32[96,512]{1,0:T(8,128)S(1)} collective-permute-done((f32[96,512]{1,0:T(8,128)}, f32[96,512]{1,0:T(8,128)S(1)}, u32[]{:S(2)}, u32[]{:S(2)}) %collective-permute-start.1) | collective-permute-done | bytes 196640 | tf_op jit(solution)/shard_map/ppermute | solution.py:50
  29.6 5.2 %collective-permute-done.2 = f32[96,512]{1,0:T(8,128)S(1)} collective-permute-done((f32[96,512]{1,0:T(8,128)}, f32[96,512]{1,0:T(8,128)S(1)}, u32[]{:S(2)}, u32[]{:S(2)}) %collective-permute-start.2) | collective-permute-done | bytes 196640 | tf_op jit(solution)/shard_map/ppermute | solution.py:50
  35.9 1.7 collective-permute-start.4
  37.5 2.6 %collective-permute-start.5 = (f32[24,512]{1,0:T(8,128)S(1)}, f32[24,512]{1,0:T(8,128)S(1)}, u32[]{:S(2)}, u32[]{:S(2)}) collective-permute-start(f32[24,512]{1,0:T(8,128)S(1)} %get-tuple-element.28), channel_id=1, source_target_pairs={{0,16},{1,17},{2,18},{3,19},{4,20},{5,21},{6,22},{7,23},{8,24},{9,... | collective-permute-start | bytes 147464 | tf_op jit(solution)/shard_map/ppermute | solution.py:50
  40.4 2.6 %collective-permute-done.5 = f32[24,512]{1,0:T(8,128)S(1)} collective-permute-done((f32[24,512]{1,0:T(8,128)S(1)}, f32[24,512]{1,0:T(8,128)S(1)}, u32[]{:S(2)}, u32[]{:S(2)}) %collective-permute-start.5) | collective-permute-done | bytes 49184 | tf_op jit(solution)/shard_map/ppermute | solution.py:50
  43.1 3.3 %collective-permute-done.6 = f32[24,512]{1,0:T(8,128)S(1)} collective-permute-done((f32[24,512]{1,0:T(8,128)S(1)}, f32[24,512]{1,0:T(8,128)S(1)}, u32[]{:S(2)}, u32[]{:S(2)}) %collective-permute-start.6) | collective-permute-done | bytes 49184 | tf_op jit(solution)/shard_map/ppermute | solution.py:50
  47.3 3.5 %collective-permute-start.9 = (f32[24,512]{1,0:T(8,128)S(1)}, f32[24,512]{1,0:T(8,128)S(1)}, u32[]{:S(2)}, u32[]{:S(2)}) collective-permute-start(f32[24,512]{1,0:T(8,128)S(1)} %add_add_fusion.1), channel_id=1, source_target_pairs={{0,24},{1,25},{2,26},{3,27},{4,28},{5,29},{6,30},{7,31},{8,16},{9,... | collective-permute-start | bytes 147464 | tf_op jit(solution)/shard_map/ppermute | solution.py:58
  51.5 1.9 %collective-permute-done.9 = f32[24,512]{1,0:T(8,128)S(1)} collective-permute-done((f32[24,512]{1,0:T(8,128)S(1)}, f32[24,512]{1,0:T(8,128)S(1)}, u32[]{:S(2)}, u32[]{:S(2)}) %collective-permute-start.9) | collective-permute-done | bytes 49184 | tf_op jit(solution)/shard_map/ppermute | solution.py:58
  57.1 2.2 %collective-permute-done.10 = f32[96,512]{1,0:T(8,128)S(1)} collective-permute-done((f32[96,512]{1,0:T(8,128)S(1)}, f32[96,512]{1,0:T(8,128)S(1)}, u32[]{:S(2)}, u32[]{:S(2)}) %collective-permute-start.10) | collective-permute-done | bytes 196640 | tf_op jit(solution)/shard_map/ppermute | solution.py:58
  59.2 3.6 %collective-permute-done.11 = f32[96,512]{1,0:T(8,128)S(1)} collective-permute-done((f32[96,512]{1,0:T(8,128)S(1)}, f32[96,512]{1,0:T(8,128)S(1)}, u32[]{:S(2)}, u32[]{:S(2)}) %collective-permute-start.11) | collective-permute-done | bytes 196640 | tf_op jit(solution)/shard_map/ppermute | solution.py:58
  63.1 2.3 %collective-permute-done.13 = f32[384,512]{1,0:T(8,128)S(1)} collective-permute-done((f32[384,512]{1,0:T(8,128)S(1)}, f32[384,512]{1,0:T(8,128)S(1)}, u32[]{:S(2)}, u32[]{:S(2)}) %collective-permute-start.13) | collective-permute-done | bytes 786464 | tf_op jit(solution)/shard_map/ppermute | solution.py:58
  66.4 11.7 %custom-call.22 = f32[128,128]{1,0:T(8,128)S(1)} custom-call(f32[128,128]{1,0:T(8,128)S(1)} %slice.140), custom_call_target="Cholesky" | custom-call | tf_op jit(solution)/shard_map/cholesky/custom-call.1 | solution.py:115
  80.1 9.9 %custom-call.15 = f32[1,128,128]{1,2,0:T(8,128)S(1)} custom-call(f32[1,128,128]{2,1,0:T(8,128)S(1)} %get-tuple-element.11), custom_call_target="InvertDiagBlocksLowerTriangular" | custom-call | tf_op jit(solution)/shard_map/triangular_solve | solution.py:116
  93.4 11.7 %custom-call.23 = f32[128,128]{1,0:T(8,128)S(1)} custom-call(f32[128,128]{1,0:T(8,128)S(1)} %slice.142), custom_call_target="Cholesky" | custom-call | tf_op jit(solution)/shard_map/cholesky/custom-call.1 | solution.py:115
  107.1 9.8 %custom-call.16 = f32[1,128,128]{1,2,0:T(8,128)S(1)} custom-call(f32[1,128,128]{2,1,0:T(8,128)S(1)} %get-tuple-element.9), custom_call_target="InvertDiagBlocksLowerTriangular" | custom-call | tf_op jit(solution)/shard_map/triangular_solve | solution.py:116
  119.8 11.9 %custom-call.24 = f32[128,128]{1,0:T(8,128)S(1)} custom-call(f32[128,128]{1,0:T(8,128)S(1)} %slice.145), custom_call_target="Cholesky" | custom-call | tf_op jit(solution)/shard_map/cholesky/custom-call.1 | solution.py:115
  133.7 9.8 %custom-call.17 = f32[1,128,128]{1,2,0:T(8,128)S(1)} custom-call(f32[1,128,128]{2,1,0:T(8,128)S(1)} %get-tuple-element.7), custom_call_target="InvertDiagBlocksLowerTriangular" | custom-call | tf_op jit(solution)/shard_map/triangular_solve | solution.py:116
  145.5 11.7 %custom-call.25 = f32[128,128]{1,0:T(8,128)S(1)} custom-call(f32[128,128]{1,0:T(8,128)S(1)} %slice.148), custom_call_target="Cholesky" | custom-call | tf_op jit(solution)/shard_map/cholesky/custom-call.1 | solution.py:115
  159.2 9.8 %custom-call.18 = f32[1,128,128]{1,2,0:T(8,128)S(1)} custom-call(f32[1,128,128]{2,1,0:T(8,128)S(1)} %get-tuple-element.5), custom_call_target="InvertDiagBlocksLowerTriangular" | custom-call | tf_op jit(solution)/shard_map/triangular_solve | solution.py:116
  (88 shorter events, 38.6 us)
Async XLA Ops:
  0.6 9.7 %copy-start = (bf16[4096,256]{1,0:T(8,128)(2,1)S(1)}, bf16[4096,256]{1,0:T(8,128)(2,1)}, u32[]{:S(2)}) copy-start(bf16[4096,256]{1,0:T(8,128)(2,1)} %param.8) | copy-start | bytes 6291460
  3.9 6.4 %copy-start.6 = (bf16[4096,512]{1,0:T(8,128)(2,1)S(1)}, bf16[4096,512]{1,0:T(8,128)(2,1)}, u32[]{:S(2)}) copy-start(bf16[4096,512]{1,0:T(8,128)(2,1)} %param.7) | copy-start | bytes 12582916
  14.3 1.1 copy-start.1
  15.6 2.6 %collective-permute-start = (f32[384,512]{1,0:T(8,128)S(1)}, f32[384,512]{1,0:T(8,128)}, u32[]{:S(2)}, u32[]{:S(2)}) collective-permute-start(f32[384,512]{1,0:T(8,128)S(1)} %slice_select_fusion), channel_id=1, source_target_pairs={{0,1},{1,0},{2,3},{3,2},{4,5},{5,4},{6,7},{7,6},{8,9},{9,8},{10,11... | collective-permute-start | bytes 2359304 | tf_op jit(solution)/shard_map/ppermute | solution.py:50
  20.9 8.7 %collective-permute-start.1 = (f32[96,512]{1,0:T(8,128)}, f32[96,512]{1,0:T(8,128)S(1)}, u32[]{:S(2)}, u32[]{:S(2)}) collective-permute-start(f32[96,512]{1,0:T(8,128)} %get-tuple-element.21), channel_id=1, source_target_pairs={{0,2},{1,3},{2,0},{3,1},{4,6},{5,7},{6,4},{7,5},{8,10},{9,11},{10,... | collective-permute-start | bytes 589832 | tf_op jit(solution)/shard_map/ppermute | solution.py:50
  23.7 11.1 %collective-permute-start.2 = (f32[96,512]{1,0:T(8,128)}, f32[96,512]{1,0:T(8,128)S(1)}, u32[]{:S(2)}, u32[]{:S(2)}) collective-permute-start(f32[96,512]{1,0:T(8,128)} %get-tuple-element.22), channel_id=1, source_target_pairs={{0,4},{1,5},{2,6},{3,7},{4,0},{5,1},{6,2},{7,3},{8,12},{9,13},{10,... | collective-permute-start | bytes 589832 | tf_op jit(solution)/shard_map/ppermute | solution.py:50
  25.3 9.5 %collective-permute-start.3 = (f32[96,512]{1,0:T(8,128)S(1)}, f32[96,512]{1,0:T(8,128)}, u32[]{:S(2)}, u32[]{:S(2)}) collective-permute-start(f32[96,512]{1,0:T(8,128)S(1)} %select_select_fusion.4), channel_id=1, source_target_pairs={{0,6},{1,7},{2,4},{3,5},{4,2},{5,3},{6,0},{7,1},{8,14},{9,15},{10,... | collective-permute-start | bytes 589832 | tf_op jit(solution)/shard_map/ppermute | solution.py:50
  35.9 4.5 %collective-permute-start.4 = (f32[24,512]{1,0:T(8,128)S(1)}, f32[24,512]{1,0:T(8,128)S(1)}, u32[]{:S(2)}, u32[]{:S(2)}) collective-permute-start(f32[24,512]{1,0:T(8,128)S(1)} %get-tuple-element.27), channel_id=1, source_target_pairs={{0,8},{1,9},{2,10},{3,11},{4,12},{5,13},{6,14},{7,15},{8,0},{9,1},... | collective-permute-start | bytes 147464 | tf_op jit(solution)/shard_map/ppermute | solution.py:50
  37.5 5.5 %collective-permute-start.5 = (f32[24,512]{1,0:T(8,128)S(1)}, f32[24,512]{1,0:T(8,128)S(1)}, u32[]{:S(2)}, u32[]{:S(2)}) collective-permute-start(f32[24,512]{1,0:T(8,128)S(1)} %get-tuple-element.28), channel_id=1, source_target_pairs={{0,16},{1,17},{2,18},{3,19},{4,20},{5,21},{6,22},{7,23},{8,24},{9,... | collective-permute-start | bytes 147464 | tf_op jit(solution)/shard_map/ppermute | solution.py:50
  40.1 6.2 %collective-permute-start.6 = (f32[24,512]{1,0:T(8,128)S(1)}, f32[24,512]{1,0:T(8,128)S(1)}, u32[]{:S(2)}, u32[]{:S(2)}) collective-permute-start(f32[24,512]{1,0:T(8,128)S(1)} %select_select_fusion.15), channel_id=1, source_target_pairs={{0,24},{1,25},{2,26},{3,27},{4,28},{5,29},{6,30},{7,31},{8,16},{9,... | collective-permute-start | bytes 147464 | tf_op jit(solution)/shard_map/ppermute | solution.py:50
  46.4 4.5 %collective-permute-start.7 = (f32[24,512]{1,0:T(8,128)S(1)}, f32[24,512]{1,0:T(8,128)S(1)}, u32[]{:S(2)}, u32[]{:S(2)}) collective-permute-start(f32[24,512]{1,0:T(8,128)S(1)} %add_add_fusion.1), channel_id=1, source_target_pairs={{0,8},{1,9},{2,10},{3,11},{4,12},{5,13},{6,14},{7,15},{8,0},{9,1},... | collective-permute-start | bytes 147464 | tf_op jit(solution)/shard_map/ppermute | solution.py:58
  46.5 5.1 %collective-permute-start.8 = (f32[24,512]{1,0:T(8,128)S(1)}, f32[24,512]{1,0:T(8,128)S(1)}, u32[]{:S(2)}, u32[]{:S(2)}) collective-permute-start(f32[24,512]{1,0:T(8,128)S(1)} %add_add_fusion.1), channel_id=1, source_target_pairs={{0,16},{1,17},{2,18},{3,19},{4,20},{5,21},{6,22},{7,23},{8,24},{9,... | collective-permute-start | bytes 147464 | tf_op jit(solution)/shard_map/ppermute | solution.py:58
  47.3 6.1 %collective-permute-start.9 = (f32[24,512]{1,0:T(8,128)S(1)}, f32[24,512]{1,0:T(8,128)S(1)}, u32[]{:S(2)}, u32[]{:S(2)}) collective-permute-start(f32[24,512]{1,0:T(8,128)S(1)} %add_add_fusion.1), channel_id=1, source_target_pairs={{0,24},{1,25},{2,26},{3,27},{4,28},{5,29},{6,30},{7,31},{8,16},{9,... | collective-permute-start | bytes 147464 | tf_op jit(solution)/shard_map/ppermute | solution.py:58
  53.5 5.7 %collective-permute-start.10 = (f32[96,512]{1,0:T(8,128)S(1)}, f32[96,512]{1,0:T(8,128)S(1)}, u32[]{:S(2)}, u32[]{:S(2)}) collective-permute-start(f32[96,512]{1,0:T(8,128)S(1)} %pad_maximum_fusion.3), channel_id=1, source_target_pairs={{0,2},{1,3},{2,0},{3,1},{4,6},{5,7},{6,4},{7,5},{8,10},{9,11},{10,... | collective-permute-start | bytes 589832 | tf_op jit(solution)/shard_map/ppermute | solution.py:58
  55.0 7.8 %collective-permute-start.11 = (f32[96,512]{1,0:T(8,128)S(1)}, f32[96,512]{1,0:T(8,128)S(1)}, u32[]{:S(2)}, u32[]{:S(2)}) collective-permute-start(f32[96,512]{1,0:T(8,128)S(1)} %pad_maximum_fusion.3), channel_id=1, source_target_pairs={{0,4},{1,5},{2,6},{3,7},{4,0},{5,1},{6,2},{7,3},{8,12},{9,13},{10,... | collective-permute-start | bytes 589832 | tf_op jit(solution)/shard_map/ppermute | solution.py:58
  55.6 7.2 %collective-permute-start.12 = (f32[96,512]{1,0:T(8,128)S(1)}, f32[96,512]{1,0:T(8,128)S(1)}, u32[]{:S(2)}, u32[]{:S(2)}) collective-permute-start(f32[96,512]{1,0:T(8,128)S(1)} %pad_maximum_fusion.3), channel_id=1, source_target_pairs={{0,6},{1,7},{2,4},{3,5},{4,2},{5,3},{6,0},{7,1},{8,14},{9,15},{10,... | collective-permute-start | bytes 589832 | tf_op jit(solution)/shard_map/ppermute | solution.py:58
  63.0 2.4 %collective-permute-start.13 = (f32[384,512]{1,0:T(8,128)S(1)}, f32[384,512]{1,0:T(8,128)S(1)}, u32[]{:S(2)}, u32[]{:S(2)}) collective-permute-start(f32[384,512]{1,0:T(8,128)S(1)} %pad_maximum_fusion.2), channel_id=1, source_target_pairs={{0,1},{1,0},{2,3},{3,2},{4,5},{5,4},{6,7},{7,6},{8,9},{9,8},{10,11... | collective-permute-start | bytes 2359304 | tf_op jit(solution)/shard_map/ppermute | solution.py:58
  90.1 1.4 copy-start.2
  92.4 0.9 copy-start.3
  144.1 1.4 copy-start.4
  171.3 1.9 %copy-start.5 = (f32[128,128]{1,0:T(8,128)S(1)}, f32[128,128]{1,0:T(8,128)}, u32[]{:S(2)}) copy-start(f32[128,128]{1,0:T(8,128)} %get-tuple-element.6) | copy-start | bytes 196612

commit v6 on v5

--- a/solution.py
+++ b/solution.py
@@ -45,17 +45,18 @@
         size = cur.shape[0] // radix
         parts = [cur[t * size : (t + 1) * size] for t in range(radix)]
         acc = pick(parts, digit)
-        for a in range(1, radix):
+        for a in sorted(range(1, radix), key=lambda a: (a != 2, a)):
             pairs = [(i, i ^ (a << k)) for i in range(n_dev)]
             acc = acc + lax.ppermute(pick(parts, digit ^ a), AXES, pairs)
         cur = acc
     for k, width in reversed(groups):
         radix = 1 << width
         digit = (idx >> k) & (radix - 1)
-        got = [cur]
-        for a in range(1, radix):
+        got = {0: cur}
+        for a in sorted(range(1, radix), key=lambda a: (a != 2, a)):
             pairs = [(i, i ^ (a << k)) for i in range(n_dev)]
-            got.append(lax.ppermute(cur, AXES, pairs))
+            got[a] = lax.ppermute(cur, AXES, pairs)
+        got = [got[a] for a in range(radix)]
         cur = jnp.concatenate([pick(got, digit ^ t) for t in range(radix)], axis=0)
     return cur
 

time: 176 us -> 177 us (level)
  transfers between devices with their start and end apart: 14 -> 14, of which waited for: 10 -> 13; matrix products, arithmetic and copies ran while one was open for 0% -> 0% of each run, Pallas kernels for 0% -> 0%
where the time goes in v6:
time: 177 us; the launch traced here: 176 us
  other arithmetic  104 us (59%)
  waiting for transfers between devices  28.7 us (16%)
  starting transfers between devices  17.6 us (10%)
  matrix products  17.5 us (10%)
  local copies, waits for them, and re-layouts  6.51 us (4%)
    another operation x12, other arithmetic, factor_and_solve(): diag = lax.linalg.cholesky(trail[:block, :block], symmetrize_input=False)  49.8 us
    another operation x8, other arithmetic, factor_and_solve(): lax.linalg.triangular_solve(diag, trail[block:, :block], left_side=False,...  44.5 us
    ppermute x7, waiting for transfers between devices, exchange_sum(): acc = acc + lax.ppermute(pick(parts, digit ^ a), AXES, pairs)  17.7 us
    ppermute x7, waiting for transfers between devices, exchange_sum(): got[a] = lax.ppermute(cur, AXES, pairs)  11 us
    ppermute x7, starting transfers between devices, exchange_sum(): acc = acc + lax.ppermute(pick(parts, digit ^ a), AXES, pairs)  9.48 us
    dot_general x2, matrix products, contract(): lax.dot_general(left, right, (((0,), (0,)), ((), ())), precision=precisio...  9 us
    ppermute x7, starting transfers between devices, exchange_sum(): got[a] = lax.ppermute(cur, AXES, pairs)  8.07 us
    unnamed x16, local copies, waits for them, and re-layouts  4.41 us
  transfers between devices with their start and end apart: 14, of which 13 were waited for; matrix products, arithmetic and copies ran while one was open for 0% of the time, Pallas kernels for 0%

profile of v6, /device:TPU:0, one launch (start us, length us, event | category | flops | bytes accessed | tf_op | source)
XLA Modules:
  0.0 176.1 jit_solution(18146215754510751514)
XLA Ops:
  3.9 6.4 %fusion.8 = f32[512,512]{1,0:T(8,128)S(1)} fusion(bf16[4096,512]{1,0:T(8,128)(2,1)} %param.7, pred[4096]{0:T(1024)(128)(4,1)S(1)} %fusion.55), kind=kOutput, calls=%fused_computation.9 | convolution fusion | flops 2149580800 | bytes 5246976 | tf_op jit(solution)/shard_map/dot_general | solution.py:11
  10.3 2.6 %fusion.11 = f32[256,512]{1,0:T(8,128)} fusion(bf16[4096,256]{1,0:T(8,128)(2,1)S(1)} %copy-done, bf16[4096,512]{1,0:T(8,128)(2,1)S(1)} %copy-done.6, pred[4096]{0:T(1024)(128)(4,1)S(1)} %fusion.55), kind=kOutput, calls=%fused_computation.10 | convolution fusion | flops 1075838976 | bytes 6819840 | tf_op jit(solution)/shard_map/dot_general | solution.py:11
  16.2 2.0 %collective-permute-done = f32[384,512]{1,0:T(8,128)} collective-permute-done((f32[384,512]{1,0:T(8,128)S(1)}, f32[384,512]{1,0:T(8,128)}, u32[]{:S(2)}, u32[]{:S(2)}) %collective-permute-start) | collective-permute-done | bytes 786464 | tf_op jit(solution)/shard_map/ppermute | solution.py:50
  18.2 1.9 %select_add_fusion = f32[384,512]{1,0:T(8,128)S(1)} fusion(f32[384,512]{1,0:T(8,128)} %collective-permute-done, f32[768,512]{1,0:T(8,128)} %copy-done.1, pred[]{:T(512)S(6)} %eq.110), kind=kLoop, calls=%fused_computation.21 | loop fusion | flops 393216 | bytes 3145729 | tf_op jit(solution)/shard_map/add | solution.py:50
  20.9 2.9 %collective-permute-start.1 = (f32[96,512]{1,0:T(8,128)}, f32[96,512]{1,0:T(8,128)S(1)}, u32[]{:S(2)}, u32[]{:S(2)}) collective-permute-start(f32[96,512]{1,0:T(8,128)} %get-tuple-element.21), channel_id=1, source_target_pairs={{0,4},{1,5},{2,6},{3,7},{4,0},{5,1},{6,2},{7,3},{8,12},{9,13},{10,... | collective-permute-start | bytes 589832 | tf_op jit(solution)/shard_map/ppermute | solution.py:50
  25.4 3.7 %collective-permute-done.1 = f32[96,512]{1,0:T(8,128)S(1)} collective-permute-done((f32[96,512]{1,0:T(8,128)}, f32[96,512]{1,0:T(8,128)S(1)}, u32[]{:S(2)}, u32[]{:S(2)}) %collective-permute-start.1) | collective-permute-done | bytes 196640 | tf_op jit(solution)/shard_map/ppermute | solution.py:50
  29.2 2.6 %collective-permute-done.2 = f32[96,512]{1,0:T(8,128)S(1)} collective-permute-done((f32[96,512]{1,0:T(8,128)}, f32[96,512]{1,0:T(8,128)S(1)}, u32[]{:S(2)}, u32[]{:S(2)}) %collective-permute-start.2) | collective-permute-done | bytes 196640 | tf_op jit(solution)/shard_map/ppermute | solution.py:50
  31.8 2.9 %collective-permute-done.3 = f32[96,512]{1,0:T(8,128)} collective-permute-done((f32[96,512]{1,0:T(8,128)S(1)}, f32[96,512]{1,0:T(8,128)}, u32[]{:S(2)}, u32[]{:S(2)}) %collective-permute-start.3) | collective-permute-done | bytes 196640 | tf_op jit(solution)/shard_map/ppermute | solution.py:50
  35.8 2.9 %collective-permute-start.4 = (f32[24,512]{1,0:T(8,128)S(1)}, f32[24,512]{1,0:T(8,128)S(1)}, u32[]{:S(2)}, u32[]{:S(2)}) collective-permute-start(f32[24,512]{1,0:T(8,128)S(1)} %get-tuple-element.27), channel_id=1, source_target_pairs={{0,16},{1,17},{2,18},{3,19},{4,20},{5,21},{6,22},{7,23},{8,24},{9,... | collective-permute-start | bytes 147464 | tf_op jit(solution)/shard_map/ppermute | solution.py:50
  40.9 1.8 %collective-permute-done.5 = f32[24,512]{1,0:T(8,128)S(1)} collective-permute-done((f32[24,512]{1,0:T(8,128)S(1)}, f32[24,512]{1,0:T(8,128)S(1)}, u32[]{:S(2)}, u32[]{:S(2)}) %collective-permute-start.5) | collective-permute-done | bytes 49184 | tf_op jit(solution)/shard_map/ppermute | solution.py:50
  42.7 4.0 %collective-permute-done.6 = f32[24,512]{1,0:T(8,128)S(1)} collective-permute-done((f32[24,512]{1,0:T(8,128)S(1)}, f32[24,512]{1,0:T(8,128)S(1)}, u32[]{:S(2)}, u32[]{:S(2)}) %collective-permute-start.6) | collective-permute-done | bytes 49184 | tf_op jit(solution)/shard_map/ppermute | solution.py:50
  47.3 4.0 %collective-permute-start.9 = (f32[24,512]{1,0:T(8,128)S(1)}, f32[24,512]{1,0:T(8,128)S(1)}, u32[]{:S(2)}, u32[]{:S(2)}) collective-permute-start(f32[24,512]{1,0:T(8,128)S(1)} %add_add_fusion.1), channel_id=1, source_target_pairs={{0,24},{1,25},{2,26},{3,27},{4,28},{5,29},{6,30},{7,31},{8,16},{9,... | collective-permute-start | bytes 147464 | tf_op jit(solution)/shard_map/ppermute | solution.py:58
  51.9 1.9 %collective-permute-done.9 = f32[24,512]{1,0:T(8,128)S(1)} collective-permute-done((f32[24,512]{1,0:T(8,128)S(1)}, f32[24,512]{1,0:T(8,128)S(1)}, u32[]{:S(2)}, u32[]{:S(2)}) %collective-permute-start.9) | collective-permute-done | bytes 49184 | tf_op jit(solution)/shard_map/ppermute | solution.py:58
  57.4 2.2 %collective-permute-done.10 = f32[96,512]{1,0:T(8,128)S(1)} collective-permute-done((f32[96,512]{1,0:T(8,128)S(1)}, f32[96,512]{1,0:T(8,128)S(1)}, u32[]{:S(2)}, u32[]{:S(2)}) %collective-permute-start.10) | collective-permute-done | bytes 196640 | tf_op jit(solution)/shard_map/ppermute | solution.py:58
  59.6 2.7 %collective-permute-done.11 = f32[96,512]{1,0:T(8,128)S(1)} collective-permute-done((f32[96,512]{1,0:T(8,128)S(1)}, f32[96,512]{1,0:T(8,128)S(1)}, u32[]{:S(2)}, u32[]{:S(2)}) %collective-permute-start.11) | collective-permute-done | bytes 196640 | tf_op jit(solution)/shard_map/ppermute | solution.py:58
  63.8 2.3 %collective-permute-done.13 = f32[384,512]{1,0:T(8,128)S(1)} collective-permute-done((f32[384,512]{1,0:T(8,128)S(1)}, f32[384,512]{1,0:T(8,128)S(1)}, u32[]{:S(2)}, u32[]{:S(2)}) %collective-permute-start.13) | collective-permute-done | bytes 786464 | tf_op jit(solution)/shard_map/ppermute | solution.py:58
  67.2 11.7 %custom-call.22 = f32[128,128]{1,0:T(8,128)S(1)} custom-call(f32[128,128]{1,0:T(8,128)S(1)} %slice.140), custom_call_target="Cholesky" | custom-call | tf_op jit(solution)/shard_map/cholesky/custom-call.1 | solution.py:116
  80.8 9.9 %custom-call.15 = f32[1,128,128]{1,2,0:T(8,128)S(1)} custom-call(f32[1,128,128]{2,1,0:T(8,128)S(1)} %get-tuple-element.11), custom_call_target="InvertDiagBlocksLowerTriangular" | custom-call | tf_op jit(solution)/shard_map/triangular_solve | solution.py:117
  94.1 11.7 %custom-call.23 = f32[128,128]{1,0:T(8,128)S(1)} custom-call(f32[128,128]{1,0:T(8,128)S(1)} %slice.142), custom_call_target="Cholesky" | custom-call | tf_op jit(solution)/shard_map/cholesky/custom-call.1 | solution.py:116
  107.8 9.8 %custom-call.16 = f32[1,128,128]{1,2,0:T(8,128)S(1)} custom-call(f32[1,128,128]{2,1,0:T(8,128)S(1)} %get-tuple-element.9), custom_call_target="InvertDiagBlocksLowerTriangular" | custom-call | tf_op jit(solution)/shard_map/triangular_solve | solution.py:117
  120.6 11.9 %custom-call.24 = f32[128,128]{1,0:T(8,128)S(1)} custom-call(f32[128,128]{1,0:T(8,128)S(1)} %slice.145), custom_call_target="Cholesky" | custom-call | tf_op jit(solution)/shard_map/cholesky/custom-call.1 | solution.py:116
  134.4 9.8 %custom-call.17 = f32[1,128,128]{1,2,0:T(8,128)S(1)} custom-call(f32[1,128,128]{2,1,0:T(8,128)S(1)} %get-tuple-element.7), custom_call_target="InvertDiagBlocksLowerTriangular" | custom-call | tf_op jit(solution)/shard_map/triangular_solve | solution.py:117
  146.3 11.7 %custom-call.25 = f32[128,128]{1,0:T(8,128)S(1)} custom-call(f32[128,128]{1,0:T(8,128)S(1)} %slice.148), custom_call_target="Cholesky" | custom-call | tf_op jit(solution)/shard_map/cholesky/custom-call.1 | solution.py:116
  160.0 9.8 %custom-call.18 = f32[1,128,128]{1,2,0:T(8,128)S(1)} custom-call(f32[1,128,128]{2,1,0:T(8,128)S(1)} %get-tuple-element.5), custom_call_target="InvertDiagBlocksLowerTriangular" | custom-call | tf_op jit(solution)/shard_map/triangular_solve | solution.py:117
  (88 shorter events, 41.3 us)
Async XLA Ops:
  0.6 9.7 %copy-start = (bf16[4096,256]{1,0:T(8,128)(2,1)S(1)}, bf16[4096,256]{1,0:T(8,128)(2,1)}, u32[]{:S(2)}) copy-start(bf16[4096,256]{1,0:T(8,128)(2,1)} %param.8) | copy-start | bytes 6291460
  3.9 6.4 %copy-start.6 = (bf16[4096,512]{1,0:T(8,128)(2,1)S(1)}, bf16[4096,512]{1,0:T(8,128)(2,1)}, u32[]{:S(2)}) copy-start(bf16[4096,512]{1,0:T(8,128)(2,1)} %param.7) | copy-start | bytes 12582916
  14.3 1.1 copy-start.1
  15.6 2.6 %collective-permute-start = (f32[384,512]{1,0:T(8,128)S(1)}, f32[384,512]{1,0:T(8,128)}, u32[]{:S(2)}, u32[]{:S(2)}) collective-permute-start(f32[384,512]{1,0:T(8,128)S(1)} %slice_select_fusion), channel_id=1, source_target_pairs={{0,1},{1,0},{2,3},{3,2},{4,5},{5,4},{6,7},{7,6},{8,9},{9,8},{10,11... | collective-permute-start | bytes 2359304 | tf_op jit(solution)/shard_map/ppermute | solution.py:50
  20.9 8.3 %collective-permute-start.1 = (f32[96,512]{1,0:T(8,128)}, f32[96,512]{1,0:T(8,128)S(1)}, u32[]{:S(2)}, u32[]{:S(2)}) collective-permute-start(f32[96,512]{1,0:T(8,128)} %get-tuple-element.21), channel_id=1, source_target_pairs={{0,4},{1,5},{2,6},{3,7},{4,0},{5,1},{6,2},{7,3},{8,12},{9,13},{10,... | collective-permute-start | bytes 589832 | tf_op jit(solution)/shard_map/ppermute | solution.py:50
  23.8 8.0 %collective-permute-start.2 = (f32[96,512]{1,0:T(8,128)}, f32[96,512]{1,0:T(8,128)S(1)}, u32[]{:S(2)}, u32[]{:S(2)}) collective-permute-start(f32[96,512]{1,0:T(8,128)} %get-tuple-element.22), channel_id=1, source_target_pairs={{0,2},{1,3},{2,0},{3,1},{4,6},{5,7},{6,4},{7,5},{8,10},{9,11},{10,... | collective-permute-start | bytes 589832 | tf_op jit(solution)/shard_map/ppermute | solution.py:50
  25.3 9.4 %collective-permute-start.3 = (f32[96,512]{1,0:T(8,128)S(1)}, f32[96,512]{1,0:T(8,128)}, u32[]{:S(2)}, u32[]{:S(2)}) collective-permute-start(f32[96,512]{1,0:T(8,128)S(1)} %select_select_fusion.4), channel_id=1, source_target_pairs={{0,6},{1,7},{2,4},{3,5},{4,2},{5,3},{6,0},{7,1},{8,14},{9,15},{10,... | collective-permute-start | bytes 589832 | tf_op jit(solution)/shard_map/ppermute | solution.py:50
  35.8 5.2 %collective-permute-start.4 = (f32[24,512]{1,0:T(8,128)S(1)}, f32[24,512]{1,0:T(8,128)S(1)}, u32[]{:S(2)}, u32[]{:S(2)}) collective-permute-start(f32[24,512]{1,0:T(8,128)S(1)} %get-tuple-element.27), channel_id=1, source_target_pairs={{0,16},{1,17},{2,18},{3,19},{4,20},{5,21},{6,22},{7,23},{8,24},{9,... | collective-permute-start | bytes 147464 | tf_op jit(solution)/shard_map/ppermute | solution.py:50
  38.6 4.1 %collective-permute-start.5 = (f32[24,512]{1,0:T(8,128)S(1)}, f32[24,512]{1,0:T(8,128)S(1)}, u32[]{:S(2)}, u32[]{:S(2)}) collective-permute-start(f32[24,512]{1,0:T(8,128)S(1)} %get-tuple-element.28), channel_id=1, source_target_pairs={{0,8},{1,9},{2,10},{3,11},{4,12},{5,13},{6,14},{7,15},{8,0},{9,1},... | collective-permute-start | bytes 147464 | tf_op jit(solution)/shard_map/ppermute | solution.py:50
  40.2 6.5 %collective-permute-start.6 = (f32[24,512]{1,0:T(8,128)S(1)}, f32[24,512]{1,0:T(8,128)S(1)}, u32[]{:S(2)}, u32[]{:S(2)}) collective-permute-start(f32[24,512]{1,0:T(8,128)S(1)} %select_select_fusion.15), channel_id=1, source_target_pairs={{0,24},{1,25},{2,26},{3,27},{4,28},{5,29},{6,30},{7,31},{8,16},{9,... | collective-permute-start | bytes 147464 | tf_op jit(solution)/shard_map/ppermute | solution.py:50
  46.8 4.5 %collective-permute-start.7 = (f32[24,512]{1,0:T(8,128)S(1)}, f32[24,512]{1,0:T(8,128)S(1)}, u32[]{:S(2)}, u32[]{:S(2)}) collective-permute-start(f32[24,512]{1,0:T(8,128)S(1)} %add_add_fusion.1), channel_id=1, source_target_pairs={{0,8},{1,9},{2,10},{3,11},{4,12},{5,13},{6,14},{7,15},{8,0},{9,1},... | collective-permute-start | bytes 147464 | tf_op jit(solution)/shard_map/ppermute | solution.py:58
  46.9 5.1 %collective-permute-start.8 = (f32[24,512]{1,0:T(8,128)S(1)}, f32[24,512]{1,0:T(8,128)S(1)}, u32[]{:S(2)}, u32[]{:S(2)}) collective-permute-start(f32[24,512]{1,0:T(8,128)S(1)} %add_add_fusion.1), channel_id=1, source_target_pairs={{0,16},{1,17},{2,18},{3,19},{4,20},{5,21},{6,22},{7,23},{8,24},{9,... | collective-permute-start | bytes 147464 | tf_op jit(solution)/shard_map/ppermute | solution.py:58
  47.3 6.5 %collective-permute-start.9 = (f32[24,512]{1,0:T(8,128)S(1)}, f32[24,512]{1,0:T(8,128)S(1)}, u32[]{:S(2)}, u32[]{:S(2)}) collective-permute-start(f32[24,512]{1,0:T(8,128)S(1)} %add_add_fusion.1), channel_id=1, source_target_pairs={{0,24},{1,25},{2,26},{3,27},{4,28},{5,29},{6,30},{7,31},{8,16},{9,... | collective-permute-start | bytes 147464 | tf_op jit(solution)/shard_map/ppermute | solution.py:58
  53.9 5.7 %collective-permute-start.10 = (f32[96,512]{1,0:T(8,128)S(1)}, f32[96,512]{1,0:T(8,128)S(1)}, u32[]{:S(2)}, u32[]{:S(2)}) collective-permute-start(f32[96,512]{1,0:T(8,128)S(1)} %pad_maximum_fusion.3), channel_id=1, source_target_pairs={{0,2},{1,3},{2,0},{3,1},{4,6},{5,7},{6,4},{7,5},{8,10},{9,11},{10,... | collective-permute-start | bytes 589832 | tf_op jit(solution)/shard_map/ppermute | solution.py:58
  55.4 6.9 %collective-permute-start.11 = (f32[96,512]{1,0:T(8,128)S(1)}, f32[96,512]{1,0:T(8,128)S(1)}, u32[]{:S(2)}, u32[]{:S(2)}) collective-permute-start(f32[96,512]{1,0:T(8,128)S(1)} %pad_maximum_fusion.3), channel_id=1, source_target_pairs={{0,4},{1,5},{2,6},{3,7},{4,0},{5,1},{6,2},{7,3},{8,12},{9,13},{10,... | collective-permute-start | bytes 589832 | tf_op jit(solution)/shard_map/ppermute | solution.py:58
  57.0 6.6 %collective-permute-start.12 = (f32[96,512]{1,0:T(8,128)S(1)}, f32[96,512]{1,0:T(8,128)S(1)}, u32[]{:S(2)}, u32[]{:S(2)}) collective-permute-start(f32[96,512]{1,0:T(8,128)S(1)} %pad_maximum_fusion.3), channel_id=1, source_target_pairs={{0,6},{1,7},{2,4},{3,5},{4,2},{5,3},{6,0},{7,1},{8,14},{9,15},{10,... | collective-permute-start | bytes 589832 | tf_op jit(solution)/shard_map/ppermute | solution.py:58
  63.7 2.4 %collective-permute-start.13 = (f32[384,512]{1,0:T(8,128)S(1)}, f32[384,512]{1,0:T(8,128)S(1)}, u32[]{:S(2)}, u32[]{:S(2)}) collective-permute-start(f32[384,512]{1,0:T(8,128)S(1)} %pad_maximum_fusion.2), channel_id=1, source_target_pairs={{0,1},{1,0},{2,3},{3,2},{4,5},{5,4},{6,7},{7,6},{8,9},{9,8},{10,11... | collective-permute-start | bytes 2359304 | tf_op jit(solution)/shard_map/ppermute | solution.py:58
  90.8 1.4 copy-start.2
  93.2 0.9 copy-start.3
  144.9 1.4 copy-start.4
  172.0 1.9 %copy-start.5 = (f32[128,128]{1,0:T(8,128)S(1)}, f32[128,128]{1,0:T(8,128)}, u32[]{:S(2)}) copy-start(f32[128,128]{1,0:T(8,128)} %get-tuple-element.6) | copy-start | bytes 196612
